TPU v7x, 128 devices: a whole 4x4x4 slice. The times are simulated.
128 devices in a mesh: dp: 8 (over z, core), fsdp: 16 (over x, y).
Axes of the slice: x: 4, y: 4, z: 4, core: 2. Of those that a mesh axis runs over, the one named last changes fastest.
Arguments:
- hidden: bfloat16 [98304, 8192], P(('dp', 'fsdp')), may hold values from -24 to 24
- head: bfloat16 [512, 8192], P('fsdp'), may hold values from -0.0625 to 0.0625
- labels: int32 [98304], P(('dp', 'fsdp')), may hold values from 0 to 511
- lse: float32 [98304], P(('dp', 'fsdp')), may hold values from 0 to 1.5
- cotangent: float32 [98304], P(('dp', 'fsdp')), may hold values from -0.6 to 0.6
- block_lists: int32 [768, 4], P(('dp', 'fsdp')), may hold values from -1 to 3, as said below
Outputs:
- grad_hidden: bfloat16 [98304, 8192], P(('dp', 'fsdp'))
- grad_head: bfloat16 [512, 8192], P('fsdp', 'dp')
Inputs may be any that keep to these rules, and one draw needn't show every extreme that they name: `block_lists`: each row names distinct vocabulary blocks in its first slots (at least one) and -1 in the remaining slots.
All inputs are finite; a program needn't handle non-finite values.
Results may differ from a plain program's by a relative error of at most 0.0056.
Values may be sent and summed in bfloat16 or wider, within the bound.
No kernel may reach another device: no remote copies, remote signals or barrier semaphores. Data moves between devices by JAX's collectives and lax.ppermute only.
A program may use at most 192 MiB of HBM per device.

v0:
```python
import jax
import jax.numpy as jnp
from jax import lax
from jax.sharding import PartitionSpec as P

VB = 128
TB = 128
VBLOCKS = 4


def on_device(hidden, head, labels, lse, cotangent, block_lists):
    blocks_here = block_lists.shape[0]
    vocab = VB * VBLOCKS
    block_ids = jnp.arange(VBLOCKS, dtype=jnp.int32)
    listed = jnp.any(block_lists[:, :, None] == block_ids[None, None, :], axis=1)
    listed_tokens = jnp.repeat(listed, TB, axis=0)
    full_head = lax.all_gather(head, "fsdp", axis=0, tiled=True)
    label_block = labels // VB
    label_listed = jnp.any(
        jnp.logical_and(label_block[:, None] == block_ids[None, :], listed_tokens), axis=1
    )
    extra = jnp.where(label_listed, 0.0, -cotangent).astype(jnp.bfloat16).astype(jnp.float32)
    label_rows = jnp.take(full_head, labels, axis=0)
    grad_acc = extra[:, None] * label_rows.astype(jnp.float32)
    vocab_ids = jnp.arange(vocab, dtype=jnp.int32)
    scaled_hits = jnp.where(vocab_ids[:, None] == labels[None, :], extra[None, :], 0.0).astype(
        jnp.bfloat16
    )
    term_acc = jnp.dot(scaled_hits, hidden, preferred_element_type=jnp.float32)

    def block_pass(block_index, carry):
        grad_all, term_all = carry
        first = block_index * TB
        rows_here = lax.dynamic_slice_in_dim(hidden, first, TB, 0)
        targets = lax.dynamic_slice_in_dim(labels, first, TB, 0)
        norms = lax.dynamic_slice_in_dim(lse, first, TB, 0)
        scales = lax.dynamic_slice_in_dim(cotangent, first, TB, 0)
        grad_rows = lax.dynamic_slice_in_dim(grad_all, first, TB, 0)
        entries = block_lists[block_index]
        count = jnp.sum((entries >= 0).astype(jnp.int32))

        def tile_pass(slot, inner):
            grad_here, term_here = inner
            vocab_block = entries[slot]
            offset = vocab_block * VB
            head_rows = lax.dynamic_slice_in_dim(full_head, offset, VB, 0)
            logits = lax.dot_general(
                rows_here, head_rows, (((1,), (1,)), ((), ())), preferred_element_type=jnp.float32
            )
            columns = offset + jnp.arange(VB, dtype=jnp.int32)
            hits = (targets[:, None] == columns[None, :]).astype(jnp.float32)
            grad_logits = (scales[:, None] * (jnp.exp(logits - norms[:, None]) - hits)).astype(
                jnp.bfloat16
            )
            grad_here = grad_here + jnp.dot(
                grad_logits, head_rows, preferred_element_type=jnp.float32
            )
            update = lax.dot_general(
                grad_logits, rows_here, (((0,), (0,)), ((), ())), preferred_element_type=jnp.float32
            )
            previous = lax.dynamic_slice_in_dim(term_here, offset, VB, 0)
            term_here = lax.dynamic_update_slice_in_dim(term_here, previous + update, offset, 0)
            return (grad_here, term_here)

        grad_rows, term_all = lax.fori_loop(0, count, tile_pass, (grad_rows, term_all))
        grad_all = lax.dynamic_update_slice_in_dim(grad_all, grad_rows, first, 0)
        return (grad_all, term_all)

    grad_acc, term_acc = lax.fori_loop(0, blocks_here, block_pass, (grad_acc, term_acc))
    grad_hidden = grad_acc.astype(jnp.bfloat16)
    slab_part = lax.psum_scatter(term_acc, "fsdp", scatter_dimension=0, tiled=True)
    owned = lax.psum_scatter(slab_part, "dp", scatter_dimension=1, tiled=True)
    return (grad_hidden, owned.astype(jnp.bfloat16))


def solution(mesh):
    return jax.shard_map(
        on_device,
        mesh=mesh,
        in_specs=(
            P(("dp", "fsdp"), None),
            P("fsdp", None),
            P(("dp", "fsdp")),
            P(("dp", "fsdp")),
            P(("dp", "fsdp")),
            P(("dp", "fsdp"), None),
        ),
        out_specs=(P(("dp", "fsdp"), None), P("fsdp", "dp")),
        check_vma=False,
    )
```

profile of v0, /device:TPU:0, one launch (start us, length us, event | category | flops | bytes accessed | tf_op | source)
XLA Modules:
  0.0 715.3 jit_solution(3298723049618193056)
XLA Ops:
  11.7 14.7 %fusion.26 = f32[512,8192]{1,0:T(8,128)} fusion(bf16[768,8192]{1,0:T(8,128)(2,1)} %param.10, f32[768]{0:T(1024)S(1)} %fusion.36, s32[768]{0:T(1024)} %param.12), kind=kOutput, calls=%fused_computation.26 | convolution fusion | flops 6443237376 | bytes 29366272 | tf_op jit(solution)/shard_map/dot_general | solution.py:29
  26.4 56.9 %all-gather.2.cloned.1.call-done = bf16[512,8192]{1,0:T(8,128)(2,1)} async-done(((bf16[32,8192]{1,0:T(8,128)(2,1)}), bf16[512,8192]{1,0:T(8,128)(2,1)}) %all-gather.2.cloned.1.call-update) | async-done | bytes 8388624 | tf_op jit(solution)/shard_map/all_gather | solution.py:17
  83.3 26.5 %gather_fusion = bf16[768,8192]{1,0:T(8,128)(2,1)} fusion(bf16[512,8192]{1,0:T(8,128)(2,1)} %all-gather.2.cloned.1.call-done, s32[1024]{0:T(1024)S(1)} %pad_clamp_fusion), kind=kCustom, calls=%fused_computation | custom fusion | bytes 25168896 | tf_op jit(solution)/shard_map/jit(_take)/gather | solution.py:23
  109.8 14.6 %convert_multiply_fusion = f32[768,8192]{1,0:T(8,128)} fusion(bf16[768,8192]{1,0:T(8,128)(2,1)} %gather_fusion, f32[768]{0:T(1024)S(1)} %fusion.36, pred[768]{0:T(1024)(128)(4,1)S(1)} %compare_and_fusion), kind=kLoop, calls=%fused_computation.23 | loop fusion | flops 18874368 | bytes 37752576 | tf_op jit(solution)/shard_map/mul | solution.py:24
  124.4 204.7 %while.42 = (s32[]{:T(128)}, f32[768,8192]{1,0:T(8,128)}, f32[512,8192]{1,0:T(8,128)}, s32[6,4]{1,0:T(8,128)S(1)}, bf16[768,8192]{1,0:T(8,128)(2,1)}, /*index=5*...) while((s32[]{:T(128)}, f32[768,8192]{1,0:T(8,128)}, ...), condition=%wide.region_6.7_spmd, body=%wide.region_2.0_spmd.sunk | while | flops 807501952 | bytes 46241948 | solution.py:69
  129.1 4.6 constant_dynamic-slice_fusion.5
  133.7 15.4 %while.43 = (s32[]{:T(128)}, f32[128,8192]{1,0:T(8,128)}, f32[512,8192]{1,0:T(8,128)}, s32[]{:T(128)}, f32[128]{0:T(128)S(1)}, /*index=5*/s32[4]{0:T(128)S(1)}, ...) while((s32[]{:T(128)}, f32[128,8192]{1,0:T(8,128)}, ...), condition=%wide.region_5.5_spmd, body=%wide.region_4.4_spmd.sunk | while | flops 807501952 | bytes 25266944 | solution.py:65
  138.0 5.6 convolution_add_fusion.3
  143.6 4.9 fusion.61
  149.1 4.5 constant_dynamic-update-slice_fusion.2
  158.3 4.6 constant_dynamic-slice_fusion.5
  162.9 30.2 %while.43 = (s32[]{:T(128)}, f32[128,8192]{1,0:T(8,128)}, f32[512,8192]{1,0:T(8,128)}, s32[]{:T(128)}, f32[128]{0:T(128)S(1)}, /*index=5*/s32[4]{0:T(128)S(1)}, ...) while((s32[]{:T(128)}, f32[128,8192]{1,0:T(8,128)}, ...), condition=%wide.region_5.5_spmd, body=%wide.region_4.4_spmd.sunk | while | flops 807501952 | bytes 25266944 | solution.py:65
  164.9 2.3 fusion.60
  167.2 5.6 convolution_add_fusion.3
  172.8 4.9 fusion.61
  179.6 2.3 fusion.60
  182.0 5.6 convolution_add_fusion.3
  187.5 4.9 fusion.61
  193.1 4.6 constant_dynamic-update-slice_fusion.2
  202.3 4.6 constant_dynamic-slice_fusion.5
  206.9 15.3 %while.43 = (s32[]{:T(128)}, f32[128,8192]{1,0:T(8,128)}, f32[512,8192]{1,0:T(8,128)}, s32[]{:T(128)}, f32[128]{0:T(128)S(1)}, /*index=5*/s32[4]{0:T(128)S(1)}, ...) while((s32[]{:T(128)}, f32[128,8192]{1,0:T(8,128)}, ...), condition=%wide.region_5.5_spmd, body=%wide.region_4.4_spmd.sunk | while | flops 807501952 | bytes 25266944 | solution.py:65
  208.9 2.3 fusion.60
  211.2 5.6 convolution_add_fusion.3
  216.8 4.8 fusion.61
  222.3 4.6 constant_dynamic-update-slice_fusion.2
  231.5 4.6 constant_dynamic-slice_fusion.5
  236.1 30.1 %while.43 = (s32[]{:T(128)}, f32[128,8192]{1,0:T(8,128)}, f32[512,8192]{1,0:T(8,128)}, s32[]{:T(128)}, f32[128]{0:T(128)S(1)}, /*index=5*/s32[4]{0:T(128)S(1)}, ...) while((s32[]{:T(128)}, f32[128,8192]{1,0:T(8,128)}, ...), condition=%wide.region_5.5_spmd, body=%wide.region_4.4_spmd.sunk | while | flops 807501952 | bytes 25266944 | solution.py:65
  238.1 2.3 fusion.60
  240.4 5.6 convolution_add_fusion.3
  246.0 4.8 fusion.61
  252.8 2.3 fusion.60
  255.1 5.6 convolution_add_fusion.3
  260.7 4.9 fusion.61
  266.2 4.6 constant_dynamic-update-slice_fusion.2
  275.4 4.6 constant_dynamic-slice_fusion.5
  280.0 15.4 %while.43 = (s32[]{:T(128)}, f32[128,8192]{1,0:T(8,128)}, f32[512,8192]{1,0:T(8,128)}, s32[]{:T(128)}, f32[128]{0:T(128)S(1)}, /*index=5*/s32[4]{0:T(128)S(1)}, ...) while((s32[]{:T(128)}, f32[128,8192]{1,0:T(8,128)}, ...), condition=%wide.region_5.5_spmd, body=%wide.region_4.4_spmd.sunk | while | flops 807501952 | bytes 25266944 | solution.py:65
  282.0 2.3 fusion.60
  284.3 5.6 convolution_add_fusion.3
  289.9 4.9 fusion.61
  295.4 4.5 constant_dynamic-update-slice_fusion.2
  304.6 4.6 constant_dynamic-slice_fusion.5
  309.2 15.3 %while.43 = (s32[]{:T(128)}, f32[128,8192]{1,0:T(8,128)}, f32[512,8192]{1,0:T(8,128)}, s32[]{:T(128)}, f32[128]{0:T(128)S(1)}, /*index=5*/s32[4]{0:T(128)S(1)}, ...) while((s32[]{:T(128)}, f32[128,8192]{1,0:T(8,128)}, ...), condition=%wide.region_5.5_spmd, body=%wide.region_4.4_spmd.sunk | while | flops 807501952 | bytes 25266944 | solution.py:65
  313.5 5.6 convolution_add_fusion.3
  319.1 4.8 fusion.61
  324.6 4.6 constant_dynamic-update-slice_fusion.2
  329.2 343.9 %reduce-scatter.3.cloned.1.call-done = f32[32,8192]{1,0:T(8,128)} async-done(((f32[512,8192]{1,0:T(8,128)}), f32[32,8192]{1,0:T(8,128)}) %reduce-scatter.3.cloned.1.call-update) | async-done | bytes 1048592 | tf_op jit(solution)/shard_map/reduce_scatter | solution.py:71
  673.2 13.2 %convert_element_type.35 = bf16[768,8192]{1,0:T(8,128)(2,1)} convert(f32[768,8192]{1,0:T(8,128)} %get-tuple-element.213) | non-fusion elementwise | flops 6291456 | bytes 37748736 | tf_op jit(solution)/shard_map/convert_element_type | solution.py:70
  686.4 20.9 %reduce-scatter.5.cloned.1.call-done = f32[32,1024]{1,0:T(8,128)} async-done(((f32[32,8192]{1,0:T(8,128)}), f32[32,1024]{1,0:T(8,128)}) %reduce-scatter.5.cloned.1.call-update) | async-done | bytes 131088 | tf_op jit(solution)/shard_map/reduce_scatter | solution.py:72
  (63 shorter events, 44.0 us)
Async XLA Ops:
  7.2 76.1 %all-gather.2.cloned.1.call-start = ((), (), s32[]{:S(2)}) async-start(), calls=%async_computation.2 | async-start | bytes 8912896 | tf_op jit(solution)/shard_map/all_gather | solution.py:17
  7.9 665.2 %reduce-scatter.3.cloned.1.call-start = ((), (), s32[]{:S(2)}) async-start(), calls=%async_computation.3 | async-start | bytes 17825792 | tf_op jit(solution)/shard_map/reduce_scatter | solution.py:71
  329.2 378.1 %reduce-scatter.5.cloned.1.call-start = ((), (), s32[]{:S(2)}) async-start(), calls=%async_computation.4 | async-start | bytes 1179648 | tf_op jit(solution)/shard_map/reduce_scatter | solution.py:72
Sparse Core Ops, SparseCore 0:
  10.1 73.1 all-gather.1
  329.3 343.8 reduce-scatter.2
  675.5 31.6 reduce-scatter.4
where the time goes:
time: 719 us; the launch traced here: 715 us
  waiting for transfers between devices  422 us (59%)
  matrix products  117 us (16%)
  local copies, waits for them, and re-layouts  112 us (16%)
  other arithmetic  36.3 us (5%)
  loops' own time  14.3 us (2%)
  between operations  13.7 us (2%)
    reduce_scatter x1, waiting for transfers between devices, on_device(): lax.psum_scatter(term_acc, 'fsdp', scatter_dimension=0, tiled=True)  344 us
    all_gather x1, waiting for transfers between devices, on_device(): full_head = lax.all_gather(head, 'fsdp', axis=0, tiled=True)  56.9 us
    dot_general x8, matrix products, tile_pass(): jnp.dot(grad_logits, head_rows, preferred_element_type=jnp.float32)  44.6 us
    dot_general x8, matrix products, tile_pass(): lax.dot_general(grad_logits, rows_here, (((0,), (0,)), ((), ())), preferr...  39.1 us
    dynamic_slice x6, local copies, waits for them, and re-layouts, block_pass(): grad_rows = lax.dynamic_slice_in_dim(grad_all, first, TB, 0)  27.7 us
    dynamic_update_slice x6, local copies, waits for them, and re-layouts, block_pass(): grad_all = lax.dynamic_update_slice_in_dim(grad_all, grad_rows, first, 0)  27.3 us
    gather x1, local copies, waits for them, and re-layouts, on_device(): label_rows = jnp.take(full_head, labels, axis=0)  26.5 us
    reduce_scatter x1, waiting for transfers between devices, on_device(): owned = lax.psum_scatter(slab_part, 'dp', scatter_dimension=1, tiled=True)  20.9 us
  transfers between devices with their start and end apart: 3, of which 3 were waited for; matrix products, arithmetic and copies ran while one was open for 4% of the time, Pallas kernels for 0%

commit v1 on v0

v1 whole, which is shorter than its diff:
```python
import jax
import jax.numpy as jnp
from jax import lax
from jax.sharding import PartitionSpec as P

VB = 128
TB = 128
VBLOCKS = 4


def on_device(hidden, head, labels, lse, cotangent, block_lists):
    vocab = VB * VBLOCKS
    block_ids = jnp.arange(VBLOCKS, dtype=jnp.int32)
    listed = jnp.any(block_lists[:, :, None] == block_ids[None, None, :], axis=1)
    mask = jnp.repeat(jnp.repeat(listed, TB, axis=0), VB, axis=1).astype(jnp.float32)
    full_head = lax.all_gather(head, "fsdp", axis=0, tiled=True)
    logits = lax.dot_general(
        hidden, full_head, (((1,), (1,)), ((), ())), preferred_element_type=jnp.float32
    )
    columns = jnp.arange(vocab, dtype=jnp.int32)
    hits = (labels[:, None] == columns[None, :]).astype(jnp.float32)
    grad_logits = (
        cotangent[:, None] * (mask * jnp.exp(logits - lse[:, None]) - hits)
    ).astype(jnp.bfloat16)
    grad_hidden = jnp.dot(grad_logits, full_head, preferred_element_type=jnp.float32)
    term = lax.dot_general(
        grad_logits, hidden, (((0,), (0,)), ((), ())), preferred_element_type=jnp.float32
    )
    slab_part = lax.psum_scatter(term, "fsdp", scatter_dimension=0, tiled=True)
    owned = lax.psum_scatter(slab_part, "dp", scatter_dimension=1, tiled=True)
    return (grad_hidden.astype(jnp.bfloat16), owned.astype(jnp.bfloat16))


def solution(mesh):
    return jax.shard_map(
        on_device,
        mesh=mesh,
        in_specs=(
            P(("dp", "fsdp"), None),
            P("fsdp", None),
            P(("dp", "fsdp")),
            P(("dp", "fsdp")),
            P(("dp", "fsdp")),
            P(("dp", "fsdp"), None),
        ),
        out_specs=(P(("dp", "fsdp"), None), P("fsdp", "dp")),
        check_vma=False,
    )
```

time: 719 us -> 266 us (0.37)
  waiting for transfers between devices: 422 us -> 206 us
  local copies, waits for them, and re-layouts: 112 us -> 2.58 us
  matrix products: 117 us -> 40.9 us
  other arithmetic: 36.3 us -> 2.24 us
  loops' own time: 14.3 us -> 0 us
    reduce_scatter x1, waiting for transfers between devices: 344 us -> 110 us  [on_device(): slab_part = lax.psum_scatter(term, 'fsdp', scatter_dimension=0, tiled=True)]
    dot_general x25 -> x3, matrix products: 117 us -> 40.9 us  [the longest x1 15.5 us: on_device(): lax.dot_general(grad_logits, hidden, (((0,), (0,)), ((), ())), preferred_...]
    dynamic_slice x38 -> x0, local copies, waits for them, and re-layouts: 56.9 us -> none  [the longest x6 27.7 us: block_pass(): grad_rows = lax.dynamic_slice_in_dim(grad_all, first, TB, 0)]
    dynamic_update_slice x6 -> x0, local copies, waits for them, and re-layouts: 27.3 us -> none  [block_pass(): grad_all = lax.dynamic_update_slice_in_dim(grad_all, grad_rows, first, 0)]
    gather x1 -> x0, local copies, waits for them, and re-layouts: 26.5 us -> none  [on_device(): label_rows = jnp.take(full_head, labels, axis=0)]
    all_gather x1, waiting for transfers between devices: 56.9 us -> 74.5 us  [on_device(): full_head = lax.all_gather(head, 'fsdp', axis=0, tiled=True)]
    mul x1 -> x0, other arithmetic: 14.6 us -> none  [on_device(): grad_acc = extra[:, None] * label_rows.astype(jnp.float32)]
    another operation x7 -> x0, loops' own time: 14.3 us -> none  [the longest x6 14.2 us: block_pass(): lax.fori_loop(0, count, tile_pass, (grad_rows, term_all))]
  transfers between devices with their start and end apart: 3 -> 3, of which waited for: 3 -> 3; matrix products, arithmetic and copies ran while one was open for 4% -> 5% of each run, Pallas kernels for 0% -> 0%
where the time goes in v1:
time: 266 us
  waiting for transfers between devices  206 us (77%)
  matrix products  40.9 us (15%)
  between operations  13.8 us (5%)
    reduce_scatter x1, waiting for transfers between devices, on_device(): slab_part = lax.psum_scatter(term, 'fsdp', scatter_dimension=0, tiled=True)  110 us
    all_gather x1, waiting for transfers between devices, on_device(): full_head = lax.all_gather(head, 'fsdp', axis=0, tiled=True)  74.5 us
    reduce_scatter x1, waiting for transfers between devices, on_device(): owned = lax.psum_scatter(slab_part, 'dp', scatter_dimension=1, tiled=True)  20.6 us
    dot_general x1, matrix products, on_device(): lax.dot_general(grad_logits, hidden, (((0,), (0,)), ((), ())), preferred_...  15.5 us
    dot_general x1, matrix products, on_device(): jnp.dot(grad_logits, full_head, preferred_element_type=jnp.float32)  13.6 us
    dot_general x1, matrix products, on_device(): lax.dot_general(hidden, full_head, (((1,), (1,)), ((), ())), preferred_el...  11.8 us
  transfers between devices with their start and end apart: 3, of which 3 were waited for; matrix products, arithmetic and copies ran while one was open for 5% of the time, Pallas kernels for 0%

profile of v1, /device:TPU:0, one launch (start us, length us, event | category | flops | bytes accessed | tf_op | source)
XLA Modules:
  0.0 265.9 jit_solution(15386275607624362866)
XLA Ops:
  7.2 0.0 all-gather.2.cloned.1.call-start
  7.2 0.7 all-gather.2.cloned.1.call-update
  7.9 0.0 reduce-scatter.3.cloned.1.call-start
  7.9 0.7 fusion.13
  8.6 0.1 copy.9
  8.8 0.0 copy-start
  8.8 0.0 copy-start.1
  8.8 0.0 copy-start.2
  8.8 74.5 %all-gather.2.cloned.1.call-done = bf16[512,8192]{1,0:T(8,128)(2,1)} async-done(((bf16[32,8192]{1,0:T(8,128)(2,1)}), bf16[512,8192]{1,0:T(8,128)(2,1)}) %all-gather.2.cloned.1.call-update) | async-done | bytes 8388624 | tf_op jit(solution)/shard_map/all_gather | solution.py:16
  83.3 11.8 %fusion.16 = f32[768,512]{1,0:T(8,128)S(1)} fusion(bf16[768,8192]{1,0:T(8,128)(2,1)} %param.6, bf16[512,8192]{1,0:T(8,128)(2,1)} %all-gather.2.cloned.1.call-done), kind=kOutput, calls=%fused_computation.20 | convolution fusion | flops 6442450944 | bytes 22544384 | tf_op jit(solution)/shard_map/dot_general | solution.py:17
  95.1 2.4 broadcast_in_dim.5
  97.6 0.0 copy-done
  97.6 0.0 copy-done.1
  97.6 0.0 copy-done.2
  97.6 15.5 %fusion = f32[512,8192]{1,0:T(8,128)} fusion(bf16[768,8192]{1,0:T(8,128)(2,1)} %param.6, f32[768,512]{1,0:T(8,128)S(1)} %fusion.16, pred[96,8,4,128]{3,2,1,0:T(4,128)(4,1)S(1)} %bitcast.15, s32[768]{0:T(1024)S(1)} %copy-done, f32[768]{0:T(1024)S(1)} %copy-done.1, f32[768]{0:T(1024)S(1)} %copy-done.2), kind=kOutput, calls=%fused_computation.3 | convolution fusion | flops 6445203456 | bytes 31335424 | tf_op jit(solution)/shard_map/dot_general | solution.py:26
  113.1 0.0 reduce-scatter.3.cloned.1.call-update
  113.1 0.0 reduce-scatter.5.cloned.1.call-start
  113.2 110.5 %reduce-scatter.3.cloned.1.call-done = f32[32,8192]{1,0:T(8,128)} async-done(((f32[512,8192]{1,0:T(8,128)}), f32[32,8192]{1,0:T(8,128)}) %reduce-scatter.3.cloned.1.call-update) | async-done | bytes 1048592 | tf_op jit(solution)/shard_map/reduce_scatter | solution.py:29
  223.6 0.0 reduce-scatter.5.cloned.1.call-update
  223.7 13.6 %convolution_convert_fusion = bf16[768,8192]{1,0:T(8,128)(2,1)} fusion(bf16[512,8192]{1,0:T(8,128)(2,1)} %all-gather.2.cloned.1.call-done, f32[768,512]{1,0:T(8,128)S(1)} %fusion.16, pred[96,8,4,128]{3,2,1,0:T(4,128)(4,1)S(1)} %bitcast.16, s32[768]{0:T(1024)S(1)} %copy-done, f32[768]{0:T(1024)S(1)} %copy-done.1, f32[768]{0:T(1024)S(1)} %copy-done.2), kind=kOutput, calls=%fused_computation | convolution fusion | flops 6451494912 | bytes 22946816 | tf_op jit(solution)/shard_map/dot_general | solution.py:25
  237.2 20.6 %reduce-scatter.5.cloned.1.call-done = f32[32,1024]{1,0:T(8,128)} async-done(((f32[32,8192]{1,0:T(8,128)}), f32[32,1024]{1,0:T(8,128)}) %reduce-scatter.5.cloned.1.call-update) | async-done | bytes 131088 | tf_op jit(solution)/shard_map/reduce_scatter | solution.py:30
  257.8 1.5 convert_element_type.16
  (1 shorter events, 0.0 us)
Async XLA Ops:
  7.2 76.1 %all-gather.2.cloned.1.call-start = ((), (), s32[]{:S(2)}) async-start(), calls=%async_computation.2 | async-start | bytes 8912896 | tf_op jit(solution)/shard_map/all_gather | solution.py:16
  7.9 215.7 %reduce-scatter.3.cloned.1.call-start = ((), (), s32[]{:S(2)}) async-start(), calls=%async_computation.3 | async-start | bytes 17825792 | tf_op jit(solution)/shard_map/reduce_scatter | solution.py:29
  8.8 88.8 %copy-start = (s32[768]{0:T(1024)S(1)}, s32[768]{0:T(1024)}, u32[]{:S(2)}) copy-start(s32[768]{0:T(1024)} %param.8) | copy-start | bytes 9220
  8.8 88.8 %copy-start.1 = (f32[768]{0:T(1024)S(1)}, f32[768]{0:T(1024)}, u32[]{:S(2)}) copy-start(f32[768]{0:T(1024)} %param.9) | copy-start | bytes 9220
  8.8 88.8 %copy-start.2 = (f32[768]{0:T(1024)S(1)}, f32[768]{0:T(1024)}, u32[]{:S(2)}) copy-start(f32[768]{0:T(1024)} %param.10) | copy-start | bytes 9220
  113.1 144.7 %reduce-scatter.5.cloned.1.call-start = ((), (), s32[]{:S(2)}) async-start(), calls=%async_computation.4 | async-start | bytes 1179648 | tf_op jit(solution)/shard_map/reduce_scatter | solution.py:30
Sparse Core Ops, SparseCore 0:
  10.1 73.1 all-gather.1
  113.2 110.3 reduce-scatter.2
  226.0 31.7 reduce-scatter.4

commit v2 on v1

--- a/solution.py
+++ b/solution.py
@@ -10,6 +10,13 @@
 
 def on_device(hidden, head, labels, lse, cotangent, block_lists):
     vocab = VB * VBLOCKS
+    dp = lax.axis_size("dp")
+    width = hidden.shape[1]
+    chunk = width // dp
+    d = lax.axis_index("dp")
+    core = d % 2
+    zpos = d // 2
+    rings = dp // 2
     block_ids = jnp.arange(VBLOCKS, dtype=jnp.int32)
     listed = jnp.any(block_lists[:, :, None] == block_ids[None, None, :], axis=1)
     mask = jnp.repeat(jnp.repeat(listed, TB, axis=0), VB, axis=1).astype(jnp.float32)
@@ -22,13 +29,26 @@
     grad_logits = (
         cotangent[:, None] * (mask * jnp.exp(logits - lse[:, None]) - hits)
     ).astype(jnp.bfloat16)
+    split = hidden.reshape(hidden.shape[0], rings, 2, chunk)
+    half = (hidden.shape[0], rings * chunk)
+    keep_rows = lax.dynamic_index_in_dim(split, core, axis=2, keepdims=False).reshape(half)
+    send_rows = lax.dynamic_index_in_dim(split, 1 - core, axis=2, keepdims=False).reshape(half)
+    contract = (((0,), (0,)), ((), ()))
+    parts = (vocab, rings, chunk)
+    send = lax.dot_general(grad_logits, send_rows, contract, preferred_element_type=jnp.float32)
+    keep = lax.dot_general(grad_logits, keep_rows, contract, preferred_element_type=jnp.float32)
+    send = send.reshape(parts)
+    keep = keep.reshape(parts)
+    got = lax.ppermute(send, "dp", [(i, i ^ 1) for i in range(dp)])
+    chip = keep + got
     grad_hidden = jnp.dot(grad_logits, full_head, preferred_element_type=jnp.float32)
-    term = lax.dot_general(
-        grad_logits, hidden, (((0,), (0,)), ((), ())), preferred_element_type=jnp.float32
-    )
-    slab_part = lax.psum_scatter(term, "fsdp", scatter_dimension=0, tiled=True)
-    owned = lax.psum_scatter(slab_part, "dp", scatter_dimension=1, tiled=True)
-    return (grad_hidden.astype(jnp.bfloat16), owned.astype(jnp.bfloat16))
+    part = lax.psum_scatter(chip, "fsdp", scatter_dimension=0, tiled=True)
+    ring = [(i, (i + 2) % dp) for i in range(dp)]
+    acc = lax.dynamic_index_in_dim(part, (zpos - 1) % rings, axis=1, keepdims=False)
+    for step in range(rings - 1):
+        acc = lax.ppermute(acc, "dp", ring)
+        acc = acc + lax.dynamic_index_in_dim(part, (zpos - 2 - step) % rings, axis=1, keepdims=False)
+    return (grad_hidden.astype(jnp.bfloat16), acc.astype(jnp.bfloat16))
 
 
 def solution(mesh):

time: 266 us -> 286 us (1.075)
  local copies, waits for them, and re-layouts: 2.58 us -> 119 us
  waiting for transfers between devices: 206 us -> 99.6 us
  matrix products: 40.9 us -> 44.8 us
    dynamic_slice x0 -> x3, local copies, waits for them, and re-layouts: none -> 94.3 us  [the longest x2 65.1 us: on_device(): lax.dynamic_index_in_dim(split, core, axis=2, keepdims=False).reshape(half)]
    all_gather x1, waiting for transfers between devices: 74.5 us -> 0.02 us  [on_device(): full_head = lax.all_gather(head, 'fsdp', axis=0, tiled=True)]
    reduce_scatter x2 -> x1, waiting for transfers between devices: 131 us -> 88.5 us  [on_device(): part = lax.psum_scatter(chip, 'fsdp', scatter_dimension=0, tiled=True)]
    reshape x0 -> x1, local copies, waits for them, and re-layouts: none -> 21.2 us  [on_device(): split = hidden.reshape(hidden.shape[0], rings, 2, chunk)]
    ppermute x0 -> x4, waiting for transfers between devices: none -> 10.5 us  [the longest x3 10.5 us: on_device(): acc = lax.ppermute(acc, 'dp', ring)]
    dot_general x1 -> x2, matrix products: 15.5 us -> 19.3 us  [the longest x1 12.6 us: on_device(): lax.dot_general(grad_logits, keep_rows, contract, preferred_element_type=...]
  transfers between devices with their start and end apart: 3 -> 6, of which waited for: 3 -> 3; matrix products, arithmetic and copies ran while one was open for 5% -> 46% of each run, Pallas kernels for 0% -> 0%
where the time goes in v2:
time: 286 us; the launch traced here: 283 us
  local copies, waits for them, and re-layouts  119 us (42%)
  waiting for transfers between devices  99.6 us (35%)
  matrix products  44.8 us (16%)
  between operations  14.2 us (5%)
  other arithmetic  3.41 us (1%)
    reduce_scatter x1, waiting for transfers between devices, on_device(): part = lax.psum_scatter(chip, 'fsdp', scatter_dimension=0, tiled=True)  88.5 us
    dynamic_slice x2, local copies, waits for them, and re-layouts, on_device(): lax.dynamic_index_in_dim(split, core, axis=2, keepdims=False).reshape(half)  65.1 us
    dynamic_slice x1, local copies, waits for them, and re-layouts, on_device(): lax.dynamic_index_in_dim(split, 1 - core, axis=2, keepdims=False)  29.1 us
    reshape x1, local copies, waits for them, and re-layouts, on_device(): split = hidden.reshape(hidden.shape[0], rings, 2, chunk)  21.2 us
    dot_general x1, matrix products, on_device(): jnp.dot(grad_logits, full_head, preferred_element_type=jnp.float32)  13.6 us
    dot_general x1, matrix products, on_device(): lax.dot_general(grad_logits, keep_rows, contract, preferred_element_type=...  12.6 us
    dot_general x1, matrix products, on_device(): lax.dot_general(hidden, full_head, (((1,), (1,)), ((), ())), preferred_el...  11.9 us
    ppermute x3, waiting for transfers between devices, on_device(): acc = lax.ppermute(acc, 'dp', ring)  10.5 us
  transfers between devices with their start and end apart: 6, of which 3 were waited for; matrix products, arithmetic and copies ran while one was open for 46% of the time, Pallas kernels for 0%

profile of v2, /device:TPU:0, one launch (start us, length us, event | category | flops | bytes accessed | tf_op | source)
XLA Modules:
  0.0 283.4 jit_solution(10333539850830109042)
XLA Ops:
  7.2 0.0 all-gather.2.cloned.1.call-start
  7.2 0.7 all-gather.2.cloned.1.call-update
  7.9 0.0 reduce-scatter.2.cloned.1.call-start
  8.0 21.2 %reshape.31 = bf16[768,4,2,1024]{3,2,1,0:T(2,128)(2,1)} reshape(bf16[768,8192]{1,0:T(8,128)(2,1)} %param.6) | data formatting | bytes 25165824 | tf_op jit(solution)/shard_map/reshape | solution.py:32
  29.2 35.7 %constant_dynamic-slice_fusion.1 = (bf16[768,4,1,1024]{3,2,1,0:T(2,128)(2,1)}, bf16[768,4,1,1024]{3,2,1,0:T(2,128)(2,1)}) fusion(bf16[768,4,2,1024]{3,2,1,0:T(2,128)(2,1)} %reshape.31, s32[]{:T(128)S(6)} %select_n.48, s32[]{:T(128)S(6)} %select_n.49), kind=kLoop, calls=%fused_computation.23 | loop fusion | bytes 25165832 | tf_op jit(solution)/shard_map/jit(dynamic_index_in_dim)/dynamic_slice | solution.py:34
  64.9 0.0 copy-start.1
  64.9 29.1 %copy.16 = bf16[768,4,1,1024]{0,3,1,2:T(8,128)(2,1)} copy(bf16[768,4,1,1024]{3,2,1,0:T(2,128)(2,1)} %get-tuple-element.3) | data formatting | bytes 12582912 | tf_op jit(solution)/shard_map/jit(dynamic_index_in_dim)/dynamic_slice | solution.py:35
  94.0 0.0 copy-done.1
  94.1 0.1 copy.13
  94.2 0.0 copy-start.2
  94.2 0.0 copy-start.3
  94.2 0.0 copy-start.4
  94.2 0.0 all-gather.2.cloned.1.call-done
  94.2 0.0 copy-start
  94.2 11.9 %fusion.19 = f32[768,512]{1,0:T(8,128)S(1)} fusion(bf16[768,8192]{1,0:T(8,128)(2,1)} %param.6, bf16[512,8192]{1,0:T(8,128)(2,1)} %all-gather.2.cloned.1.call-done), kind=kOutput, calls=%fused_computation.25 | convolution fusion | flops 6442450944 | bytes 22544384 | tf_op jit(solution)/shard_map/dot_general | solution.py:24
  106.2 2.4 broadcast_in_dim.5
  108.6 0.0 copy-done.2
  108.6 0.0 copy-done.3
  108.7 0.0 copy-done.4
  108.7 0.0 copy-done
  108.7 6.7 %fusion = f32[512,4,1024]{2,0,1:T(8,128)} fusion(bf16[768,4,1,1024]{0,3,1,2:T(8,128)(2,1)S(1)} %copy-done, f32[768,512]{1,0:T(8,128)S(1)} %fusion.19, pred[96,8,4,128]{3,2,1,0:T(4,128)(4,1)S(1)} %bitcast.44, s32[768]{0:T(1024)S(1)} %copy-done.2, f32[768]{0:T(1024)S(1)} %copy-done.3, f32[768]{0:T(1024)S(1)} %copy-done.4), kind=kOutput, calls=%fused_computation.1 | convolution fusion | flops 3223977984 | bytes 16655360 | tf_op jit(solution)/shard_map/dot_general | solution.py:38
  115.3 0.0 collective-permute-start
  115.3 29.4 %copy.14 = bf16[768,4,1,1024]{0,3,1,2:T(8,128)(2,1)} copy(bf16[768,4,1,1024]{3,2,1,0:T(2,128)(2,1)} %get-tuple-element.2) | data formatting | bytes 12582912 | tf_op jit(solution)/shard_map/jit(dynamic_index_in_dim)/dynamic_slice | solution.py:34
  144.7 0.0 collective-permute-done
  144.7 12.6 %fusion.4 = f32[512,4,1024]{2,0,1:T(8,128)} fusion(f32[512,4,1024]{2,0,1:T(8,128)} %collective-permute-done, bf16[768,4,1,1024]{0,3,1,2:T(8,128)(2,1)} %copy.14, f32[768,512]{1,0:T(8,128)S(1)} %fusion.19, pred[96,8,4,128]{3,2,1,0:T(4,128)(4,1)S(1)} %bitcast.45, s32[768]{0:T(1024)S(1)} %copy-done.2, f32[768]{0:T(1024)S(1)} %copy-done.3, f32[768]{0:T(1024)S(1)} %copy-done.4), kind=kOutput, calls=%fused_computation.5 | convolution fusion | flops 3226075136 | bytes 25043968 | tf_op jit(solution)/shard_map/dot_general | solution.py:39
  157.4 0.0 reduce-scatter.2.cloned.1.call-update
  157.4 88.5 %reduce-scatter.2.cloned.1.call-done = f32[32,4,1024]{2,0,1:T(8,128)} async-done(((f32[512,4,1024]{2,0,1:T(8,128)}), f32[32,4,1024]{2,0,1:T(8,128)}) %reduce-scatter.2.cloned.1.call-update) | async-done | bytes 524304 | tf_op jit(solution)/shard_map/reduce_scatter | solution.py:45
  245.9 0.9 dynamic-slice_bitcast_fusion
  246.8 1.8 collective-permute-start.1
  248.6 4.6 %collective-permute-done.1 = f32[32,1024]{1,0:T(8,128)S(1)} collective-permute-done((f32[32,1024]{1,0:T(8,128)S(1)}, f32[32,1024]{1,0:T(8,128)S(1)}, u32[]{:S(2)}, u32[]{:S(2)}) %collective-permute-start.1) | collective-permute-done | bytes 131104 | tf_op jit(solution)/shard_map/ppermute | solution.py:49
  253.3 0.9 bitcast_add_fusion.2
  254.2 0.4 collective-permute-start.2
  254.6 5.8 %collective-permute-done.2 = f32[32,1024]{1,0:T(8,128)S(1)} collective-permute-done((f32[32,1024]{1,0:T(8,128)S(1)}, f32[32,1024]{1,0:T(8,128)S(1)}, u32[]{:S(2)}, u32[]{:S(2)}) %collective-permute-start.2) | collective-permute-done | bytes 131104 | tf_op jit(solution)/shard_map/ppermute | solution.py:49
  260.4 0.9 bitcast_add_fusion.1
  261.4 0.1 collective-permute-start.3
  261.4 13.6 %convolution_convert_fusion = bf16[768,8192]{1,0:T(8,128)(2,1)} fusion(bf16[512,8192]{1,0:T(8,128)(2,1)} %all-gather.2.cloned.1.call-done, f32[768,512]{1,0:T(8,128)S(1)} %fusion.19, pred[96,8,4,128]{3,2,1,0:T(4,128)(4,1)S(1)} %bitcast.46, s32[768]{0:T(1024)S(1)} %copy-done.2, f32[768]{0:T(1024)S(1)} %copy-done.3, f32[768]{0:T(1024)S(1)} %copy-done.4), kind=kOutput, calls=%fused_computation | convolution fusion | flops 6451494912 | bytes 22946816 | tf_op jit(solution)/shard_map/dot_general | solution.py:44
  275.0 0.0 collective-permute-done.3
  275.0 1.6 fusion.14
  (2 shorter events, 0.0 us)
Async XLA Ops:
  7.2 87.0 %all-gather.2.cloned.1.call-start = ((), (), s32[]{:S(2)}) async-start(), calls=%async_computation.1 | async-start | bytes 8912896 | tf_op jit(solution)/shard_map/all_gather | solution.py:23
  7.9 238.0 %reduce-scatter.2.cloned.1.call-start = ((), (), s32[]{:S(2)}) async-start(), calls=%async_computation.2 | async-start | bytes 8912896 | tf_op jit(solution)/shard_map/reduce_scatter | solution.py:45
  64.9 29.2 %copy-start.1 = (s32[6,4]{0,1:T(4,128)S(1)}, s32[6,4]{0,1:T(4,128)}, u32[]{:S(2)}) copy-start(s32[6,4]{0,1:T(4,128)} %param.11) | copy-start | bytes 292
  94.2 14.5 %copy-start.2 = (s32[768]{0:T(1024)S(1)}, s32[768]{0:T(1024)}, u32[]{:S(2)}) copy-start(s32[768]{0:T(1024)} %param.8) | copy-start | bytes 9220
  94.2 14.5 %copy-start.3 = (f32[768]{0:T(1024)S(1)}, f32[768]{0:T(1024)}, u32[]{:S(2)}) copy-start(f32[768]{0:T(1024)} %param.9) | copy-start | bytes 9220
  94.2 14.5 %copy-start.4 = (f32[768]{0:T(1024)S(1)}, f32[768]{0:T(1024)}, u32[]{:S(2)}) copy-start(f32[768]{0:T(1024)} %param.10) | copy-start | bytes 9220
  94.2 14.5 %copy-start = (bf16[768,4,1,1024]{0,3,1,2:T(8,128)(2,1)S(1)}, bf16[768,4,1,1024]{0,3,1,2:T(8,128)(2,1)}, u32[]{:S(2)}) copy-start(bf16[768,4,1,1024]{0,3,1,2:T(8,128)(2,1)} %copy.16) | copy-start | bytes 18874372
  115.3 29.4 %collective-permute-start = (f32[512,4,1024]{2,0,1:T(8,128)}, f32[512,4,1024]{2,0,1:T(8,128)}, u32[]{:S(2)}, u32[]{:S(2)}) collective-permute-start(f32[512,4,1024]{2,0,1:T(8,128)} %fusion), channel_id=1, source_target_pairs={{0,16},{16,0},{32,48},{48,32},{64,80},{80,64},{96,112},{112,96},{1... | collective-permute-start | bytes 25165832 | tf_op jit(solution)/shard_map/ppermute | solution.py:42
  246.8 6.4 %collective-permute-start.1 = (f32[32,1024]{1,0:T(8,128)S(1)}, f32[32,1024]{1,0:T(8,128)S(1)}, u32[]{:S(2)}, u32[]{:S(2)}) collective-permute-start(f32[32,1024]{1,0:T(8,128)S(1)} %dynamic-slice_bitcast_fusion), channel_id=1, source_target_pairs={{0,32},{16,48},{32,64},{48,80},{64,96},{80,112},{96,0},{112,16},{1... | collective-permute-start | bytes 393224 | tf_op jit(solution)/shard_map/ppermute | solution.py:49
  254.2 6.2 %collective-permute-start.2 = (f32[32,1024]{1,0:T(8,128)S(1)}, f32[32,1024]{1,0:T(8,128)S(1)}, u32[]{:S(2)}, u32[]{:S(2)}) collective-permute-start(f32[32,1024]{1,0:T(8,128)S(1)} %bitcast_add_fusion.2), channel_id=1, source_target_pairs={{0,32},{16,48},{32,64},{48,80},{64,96},{80,112},{96,0},{112,16},{1... | collective-permute-start | bytes 393224 | tf_op jit(solution)/shard_map/ppermute | solution.py:49
  261.4 13.6 %collective-permute-start.3 = (f32[32,1024]{1,0:T(8,128)S(1)}, f32[32,1024]{1,0:T(8,128)S(1)}, u32[]{:S(2)}, u32[]{:S(2)}) collective-permute-start(f32[32,1024]{1,0:T(8,128)S(1)} %bitcast_add_fusion.1), channel_id=1, source_target_pairs={{0,32},{16,48},{32,64},{48,80},{64,96},{80,112},{96,0},{112,16},{1... | collective-permute-start | bytes 393224 | tf_op jit(solution)/shard_map/ppermute | solution.py:49
Sparse Core Ops, SparseCore 0:
  10.1 73.1 all-gather.1
  157.5 88.3 reduce-scatter.1

commit v3 on v2

--- a/solution.py
+++ b/solution.py
@@ -29,25 +29,30 @@
     grad_logits = (
         cotangent[:, None] * (mask * jnp.exp(logits - lse[:, None]) - hits)
     ).astype(jnp.bfloat16)
-    split = hidden.reshape(hidden.shape[0], rings, 2, chunk)
-    half = (hidden.shape[0], rings * chunk)
-    keep_rows = lax.dynamic_index_in_dim(split, core, axis=2, keepdims=False).reshape(half)
-    send_rows = lax.dynamic_index_in_dim(split, 1 - core, axis=2, keepdims=False).reshape(half)
+    def columns_of(parity):
+        picks = [
+            lax.dynamic_slice_in_dim(hidden, (2 * j + parity) * chunk, chunk, axis=1)
+            for j in range(rings)
+        ]
+        return jnp.concatenate(picks, axis=1)
+
     contract = (((0,), (0,)), ((), ()))
-    parts = (vocab, rings, chunk)
-    send = lax.dot_general(grad_logits, send_rows, contract, preferred_element_type=jnp.float32)
-    keep = lax.dot_general(grad_logits, keep_rows, contract, preferred_element_type=jnp.float32)
-    send = send.reshape(parts)
-    keep = keep.reshape(parts)
+    send = lax.dot_general(
+        grad_logits, columns_of(1 - core), contract, preferred_element_type=jnp.float32
+    )
     got = lax.ppermute(send, "dp", [(i, i ^ 1) for i in range(dp)])
+    keep = lax.dot_general(
+        grad_logits, columns_of(core), contract, preferred_element_type=jnp.float32
+    )
     chip = keep + got
     grad_hidden = jnp.dot(grad_logits, full_head, preferred_element_type=jnp.float32)
     part = lax.psum_scatter(chip, "fsdp", scatter_dimension=0, tiled=True)
     ring = [(i, (i + 2) % dp) for i in range(dp)]
-    acc = lax.dynamic_index_in_dim(part, (zpos - 1) % rings, axis=1, keepdims=False)
+    acc = lax.dynamic_slice_in_dim(part, ((zpos - 1) % rings) * chunk, chunk, axis=1)
     for step in range(rings - 1):
         acc = lax.ppermute(acc, "dp", ring)
-        acc = acc + lax.dynamic_index_in_dim(part, (zpos - 2 - step) % rings, axis=1, keepdims=False)
+        own = lax.dynamic_slice_in_dim(part, ((zpos - 2 - step) % rings) * chunk, chunk, axis=1)
+        acc = acc + own
     return (grad_hidden.astype(jnp.bfloat16), acc.astype(jnp.bfloat16))
 
 

time: 286 us -> 253 us (0.88)
  local copies, waits for them, and re-layouts: 119 us -> 12.5 us
  waiting for transfers between devices: 99.6 us -> 176 us
    dynamic_slice x3 -> x2, local copies, waits for them, and re-layouts: 94.3 us -> 9.9 us  [the longest x1 8.99 us: columns_of(): lax.dynamic_slice_in_dim(hidden, (2 * j + parity) * chunk, chunk, axis=1)]
    all_gather x1, waiting for transfers between devices: 0.02 us -> 65.5 us  [on_device(): full_head = lax.all_gather(head, 'fsdp', axis=0, tiled=True)]
    reshape x1 -> x0, local copies, waits for them, and re-layouts: 21.2 us -> none  [on_device(): split = hidden.reshape(hidden.shape[0], rings, 2, chunk)]
    ppermute x1, waiting for transfers between devices: 0.01 us -> 13.5 us  [on_device(): got = lax.ppermute(send, 'dp', [(i, i ^ 1) for i in range(dp)])]
  transfers between devices with their start and end apart: 6 -> 6, of which waited for: 3 -> 5; matrix products, arithmetic and copies ran while one was open for 46% -> 9% of each run, Pallas kernels for 0% -> 0%
where the time goes in v3:
time: 253 us
  waiting for transfers between devices  176 us (70%)
  matrix products  43.9 us (17%)
  between operations  14.3 us (6%)
  local copies, waits for them, and re-layouts  12.5 us (5%)
  other arithmetic  4.09 us (2%)
    reduce_scatter x1, waiting for transfers between devices, on_device(): part = lax.psum_scatter(chip, 'fsdp', scatter_dimension=0, tiled=True)  85.8 us
    all_gather x1, waiting for transfers between devices, on_device(): full_head = lax.all_gather(head, 'fsdp', axis=0, tiled=True)  65.5 us
    dot_general x1, matrix products, on_device(): jnp.dot(grad_logits, full_head, preferred_element_type=jnp.float32)  13.6 us
    ppermute x1, waiting for transfers between devices, on_device(): got = lax.ppermute(send, 'dp', [(i, i ^ 1) for i in range(dp)])  13.5 us
    dot_general x1, matrix products, on_device(): lax.dot_general(hidden, full_head, (((1,), (1,)), ((), ())), preferred_el...  11.9 us
    dot_general x1, matrix products, on_device(): lax.dot_general(grad_logits, columns_of(core), contract, preferred_elemen...  10.9 us
    ppermute x3, waiting for transfers between devices, on_device(): acc = lax.ppermute(acc, 'dp', ring)  10.5 us
    dynamic_slice x1, local copies, waits for them, and re-layouts, columns_of(): lax.dynamic_slice_in_dim(hidden, (2 * j + parity) * chunk, chunk, axis=1)  8.99 us
  transfers between devices with their start and end apart: 6, of which 5 were waited for; matrix products, arithmetic and copies ran while one was open for 9% of the time, Pallas kernels for 0%

profile of v3, /device:TPU:0, one launch (start us, length us, event | category | flops | bytes accessed | tf_op | source)
XLA Modules:
  0.0 253.2 jit_solution(8864394660766248485)
XLA Ops:
  7.2 0.0 all-gather.2.cloned.1.call-start
  7.2 0.7 all-gather.2.cloned.1.call-update
  7.9 0.0 reduce-scatter.2.cloned.1.call-start
  8.0 0.7 fusion.37
  8.7 0.1 copy.9
  8.8 9.0 %constant_dynamic-slice_fusion.8 = (bf16[768,1024]{1,0:T(8,128)(2,1)S(1)}, bf16[768,1024]{1,0:T(8,128)(2,1)}, bf16[768,1024]{1,0:T(8,128)(2,1)}, bf16[768,1024]{...) fusion(bf16[768,8192]{1,0:T(8,128)(2,1)} %param.6, ...), kind=kLoop, calls=%fused_computation.51 | loop fusion | bytes 25165856 | tf_op jit(solution)/shard_map/dynamic_slice | solution.py:34
  17.8 0.0 copy-start.6
  17.8 0.0 copy-start.7
  17.8 0.0 copy-start.8
  17.8 65.5 %all-gather.2.cloned.1.call-done = bf16[512,8192]{1,0:T(8,128)(2,1)} async-done(((bf16[32,8192]{1,0:T(8,128)(2,1)}), bf16[512,8192]{1,0:T(8,128)(2,1)}) %all-gather.2.cloned.1.call-update) | async-done | bytes 8388624 | tf_op jit(solution)/shard_map/all_gather | solution.py:23
  83.3 0.0 copy-start.2
  83.3 0.0 copy-start.3
  83.3 0.0 copy-start.4
  83.3 0.0 copy-start.5
  83.3 11.9 %fusion.43 = f32[768,512]{1,0:T(8,128)S(1)} fusion(bf16[768,8192]{1,0:T(8,128)(2,1)} %param.6, bf16[512,8192]{1,0:T(8,128)(2,1)} %all-gather.2.cloned.1.call-done), kind=kOutput, calls=%fused_computation.57 | convolution fusion | flops 6442450944 | bytes 22544384 | tf_op jit(solution)/shard_map/dot_general | solution.py:24
  95.2 0.0 copy-start.9
  95.3 2.4 broadcast_in_dim.5
  97.7 0.0 copy-done.6
  97.7 0.0 copy-done.7
  97.7 0.0 copy-done.8
  97.8 0.0 copy-done.2
  97.8 0.0 copy-done.3
  97.8 0.0 copy-done.4
  97.8 0.0 copy-done.5
  97.8 0.0 copy-start
  97.8 0.0 copy-start.1
  97.8 7.6 %fusion.11 = f32[512,4096]{1,0:T(8,128)} fusion(bf16[768,1024]{1,0:T(8,128)(2,1)S(1)} %copy-done.4, bf16[768,1024]{1,0:T(8,128)(2,1)S(1)} %copy-done.5, bf16[768,1024]{1,0:T(8,128)(2,1)S(1)} %copy-done.2, bf16[768,1024]{1,0:T(8,128)(2,1)S(1)} %copy-done.3, f32[768,512]{1,0:T(8,128)S(1)} %fusion.43, pred[96,8,4,128]{3,2,1,0:T(4,128)(4,1)S(1)} %bitcast.18, ...), kind=kOutput, calls=%fused_computation.10 | convolution fusion | flops 3249143808 | bytes 16655360 | tf_op jit(solution)/shard_map/dot_general | solution.py:40
  105.4 0.0 collective-permute-start
  105.4 13.5 %collective-permute-done = f32[512,4096]{1,0:T(8,128)} collective-permute-done((f32[512,4096]{1,0:T(8,128)}, f32[512,4096]{1,0:T(8,128)}, u32[]{:S(2)}, u32[]{:S(2)}) %collective-permute-start) | collective-permute-done | bytes 8388640 | tf_op jit(solution)/shard_map/ppermute | solution.py:43
  118.9 0.0 copy-done.9
  118.9 0.0 copy-done
  118.9 0.0 copy-done.1
  118.9 10.9 %fusion.2 = f32[512,4096]{1,0:T(8,128)} fusion(f32[512,4096]{1,0:T(8,128)} %collective-permute-done, bf16[768,1024]{1,0:T(8,128)(2,1)S(1)} %get-tuple-element.5, bf16[768,1024]{1,0:T(8,128)(2,1)S(1)} %copy-done, bf16[768,1024]{1,0:T(8,128)(2,1)S(1)} %copy-done.1, bf16[768,1024]{1,0:T(8,128)(2,1)S(1)} %get-tuple-element.2, f32[768,512]{1,0:T(8,128)S(1)} %fusion.43, ...), kind=kOutput, calls=%fused_computation.3 | convolution fusion | flops 3251240960 | bytes 25043968 | tf_op jit(solution)/shard_map/dot_general | solution.py:44
  129.8 0.0 copy-start.10
  129.8 0.0 reduce-scatter.2.cloned.1.call-update
  129.9 85.8 %reduce-scatter.2.cloned.1.call-done = f32[32,4096]{1,0:T(8,128)} async-done(((f32[512,4096]{1,0:T(8,128)}), f32[32,4096]{1,0:T(8,128)}) %reduce-scatter.2.cloned.1.call-update) | async-done | bytes 524304 | tf_op jit(solution)/shard_map/reduce_scatter | solution.py:49
  215.7 0.9 constant_dynamic-slice_fusion
  216.6 1.8 collective-permute-start.1
  218.4 4.6 %collective-permute-done.1 = f32[32,1024]{1,0:T(8,128)S(1)} collective-permute-done((f32[32,1024]{1,0:T(8,128)S(1)}, f32[32,1024]{1,0:T(8,128)S(1)}, u32[]{:S(2)}, u32[]{:S(2)}) %collective-permute-start.1) | collective-permute-done | bytes 131104 | tf_op jit(solution)/shard_map/ppermute | solution.py:53
  223.0 0.9 dynamic-slice_add_fusion.1
  224.0 0.4 collective-permute-start.2
  224.4 5.8 %collective-permute-done.2 = f32[32,1024]{1,0:T(8,128)S(1)} collective-permute-done((f32[32,1024]{1,0:T(8,128)S(1)}, f32[32,1024]{1,0:T(8,128)S(1)}, u32[]{:S(2)}, u32[]{:S(2)}) %collective-permute-start.2) | collective-permute-done | bytes 131104 | tf_op jit(solution)/shard_map/ppermute | solution.py:53
  230.2 0.9 dynamic-slice_add_fusion
  231.1 0.1 collective-permute-start.3
  231.2 0.0 copy-done.10
  231.2 13.6 %convolution_convert_fusion = bf16[768,8192]{1,0:T(8,128)(2,1)} fusion(bf16[512,8192]{1,0:T(8,128)(2,1)} %all-gather.2.cloned.1.call-done, f32[768,512]{1,0:T(8,128)S(1)} %copy-done.10, pred[96,8,4,128]{3,2,1,0:T(4,128)(4,1)S(1)} %bitcast.20, s32[768]{0:T(1024)S(1)} %copy-done.6, f32[768]{0:T(1024)S(1)} %copy-done.7, f32[768]{0:T(1024)S(1)} %copy-done.8), kind=kOutput, calls=%fused_computation | convolution fusion | flops 6451494912 | bytes 22946816 | tf_op jit(solution)/shard_map/dot_general | solution.py:48
  244.8 0.0 collective-permute-done.3
  244.8 1.6 add_convert_fusion
  (1 shorter events, 0.0 us)
Async XLA Ops:
  7.2 76.1 %all-gather.2.cloned.1.call-start = ((), (), s32[]{:S(2)}) async-start(), calls=%async_computation.1 | async-start | bytes 8912896 | tf_op jit(solution)/shard_map/all_gather | solution.py:23
  7.9 207.8 %reduce-scatter.2.cloned.1.call-start = ((), (), s32[]{:S(2)}) async-start(), calls=%async_computation.2 | async-start | bytes 8912896 | tf_op jit(solution)/shard_map/reduce_scatter | solution.py:49
  17.8 80.0 %copy-start.6 = (s32[768]{0:T(1024)S(1)}, s32[768]{0:T(1024)}, u32[]{:S(2)}) copy-start(s32[768]{0:T(1024)} %param.8) | copy-start | bytes 9220
  17.8 79.9 %copy-start.7 = (f32[768]{0:T(1024)S(1)}, f32[768]{0:T(1024)}, u32[]{:S(2)}) copy-start(f32[768]{0:T(1024)} %param.9) | copy-start | bytes 9220
  17.8 79.9 %copy-start.8 = (f32[768]{0:T(1024)S(1)}, f32[768]{0:T(1024)}, u32[]{:S(2)}) copy-start(f32[768]{0:T(1024)} %param.10) | copy-start | bytes 9220
  83.3 14.5 %copy-start.2 = (bf16[768,1024]{1,0:T(8,128)(2,1)S(1)}, bf16[768,1024]{1,0:T(8,128)(2,1)}, u32[]{:S(2)}) copy-start(bf16[768,1024]{1,0:T(8,128)(2,1)} %get-tuple-element.3) | copy-start | bytes 4718596
  83.3 14.5 %copy-start.3 = (bf16[768,1024]{1,0:T(8,128)(2,1)S(1)}, bf16[768,1024]{1,0:T(8,128)(2,1)}, u32[]{:S(2)}) copy-start(bf16[768,1024]{1,0:T(8,128)(2,1)} %get-tuple-element.4) | copy-start | bytes 4718596
  83.3 14.5 %copy-start.4 = (bf16[768,1024]{1,0:T(8,128)(2,1)S(1)}, bf16[768,1024]{1,0:T(8,128)(2,1)}, u32[]{:S(2)}) copy-start(bf16[768,1024]{1,0:T(8,128)(2,1)} %get-tuple-element.8) | copy-start | bytes 4718596
  83.3 14.5 %copy-start.5 = (bf16[768,1024]{1,0:T(8,128)(2,1)S(1)}, bf16[768,1024]{1,0:T(8,128)(2,1)}, u32[]{:S(2)}) copy-start(bf16[768,1024]{1,0:T(8,128)(2,1)} %get-tuple-element.9) | copy-start | bytes 4718596
  95.2 23.6 %copy-start.9 = (f32[768,512]{1,0:T(8,128)}, f32[768,512]{1,0:T(8,128)S(1)}, u32[]{:S(2)}) copy-start(f32[768,512]{1,0:T(8,128)S(1)} %fusion.43) | copy-start | bytes 4718596
  97.8 21.1 %copy-start = (bf16[768,1024]{1,0:T(8,128)(2,1)S(1)}, bf16[768,1024]{1,0:T(8,128)(2,1)}, u32[]{:S(2)}) copy-start(bf16[768,1024]{1,0:T(8,128)(2,1)} %get-tuple-element.6) | copy-start | bytes 4718596
  97.8 21.1 %copy-start.1 = (bf16[768,1024]{1,0:T(8,128)(2,1)S(1)}, bf16[768,1024]{1,0:T(8,128)(2,1)}, u32[]{:S(2)}) copy-start(bf16[768,1024]{1,0:T(8,128)(2,1)} %get-tuple-element.7) | copy-start | bytes 4718596
  105.4 13.5 %collective-permute-start = (f32[512,4096]{1,0:T(8,128)}, f32[512,4096]{1,0:T(8,128)}, u32[]{:S(2)}, u32[]{:S(2)}) collective-permute-start(f32[512,4096]{1,0:T(8,128)} %fusion.11), channel_id=1, source_target_pairs={{0,16},{16,0},{32,48},{48,32},{64,80},{80,64},{96,112},{112,96},{1... | collective-permute-start | bytes 25165832 | tf_op jit(solution)/shard_map/ppermute | solution.py:43
  129.8 101.4 %copy-start.10 = (f32[768,512]{1,0:T(8,128)S(1)}, f32[768,512]{1,0:T(8,128)}, u32[]{:S(2)}) copy-start(f32[768,512]{1,0:T(8,128)} %copy-done.9) | copy-start | bytes 4718596
  216.6 6.4 %collective-permute-start.1 = (f32[32,1024]{1,0:T(8,128)S(1)}, f32[32,1024]{1,0:T(8,128)S(1)}, u32[]{:S(2)}, u32[]{:S(2)}) collective-permute-start(f32[32,1024]{1,0:T(8,128)S(1)} %constant_dynamic-slice_fusion), channel_id=1, source_target_pairs={{0,32},{16,48},{32,64},{48,80},{64,96},{80,112},{96,0},{112,16},{1... | collective-permute-start | bytes 393224 | tf_op jit(solution)/shard_map/ppermute | solution.py:53
  224.0 6.2 %collective-permute-start.2 = (f32[32,1024]{1,0:T(8,128)S(1)}, f32[32,1024]{1,0:T(8,128)S(1)}, u32[]{:S(2)}, u32[]{:S(2)}) collective-permute-start(f32[32,1024]{1,0:T(8,128)S(1)} %dynamic-slice_add_fusion.1), channel_id=1, source_target_pairs={{0,32},{16,48},{32,64},{48,80},{64,96},{80,112},{96,0},{112,16},{1... | collective-permute-start | bytes 393224 | tf_op jit(solution)/shard_map/ppermute | solution.py:53
  231.1 13.6 %collective-permute-start.3 = (f32[32,1024]{1,0:T(8,128)S(1)}, f32[32,1024]{1,0:T(8,128)S(1)}, u32[]{:S(2)}, u32[]{:S(2)}) collective-permute-start(f32[32,1024]{1,0:T(8,128)S(1)} %dynamic-slice_add_fusion), channel_id=1, source_target_pairs={{0,32},{16,48},{32,64},{48,80},{64,96},{80,112},{96,0},{112,16},{1... | collective-permute-start | bytes 393224 | tf_op jit(solution)/shard_map/ppermute | solution.py:53
Sparse Core Ops, SparseCore 0:
  10.1 73.1 all-gather.1
  129.9 85.7 reduce-scatter.1

commit v4 on v3

--- a/solution.py
+++ b/solution.py
@@ -44,15 +44,24 @@
     keep = lax.dot_general(
         grad_logits, columns_of(core), contract, preferred_element_type=jnp.float32
     )
+    grad_hidden = jnp.dot(grad_logits, full_head, preferred_element_type=jnp.float32)
+    keep, grad_hidden = lax.optimization_barrier((keep, grad_hidden))
     chip = keep + got
-    grad_hidden = jnp.dot(grad_logits, full_head, preferred_element_type=jnp.float32)
     part = lax.psum_scatter(chip, "fsdp", scatter_dimension=0, tiled=True)
-    ring = [(i, (i + 2) % dp) for i in range(dp)]
-    acc = lax.dynamic_slice_in_dim(part, ((zpos - 1) % rings) * chunk, chunk, axis=1)
-    for step in range(rings - 1):
-        acc = lax.ppermute(acc, "dp", ring)
-        own = lax.dynamic_slice_in_dim(part, ((zpos - 2 - step) % rings) * chunk, chunk, axis=1)
-        acc = acc + own
+    def piece(k):
+        return lax.dynamic_slice_in_dim(part, (k % rings) * chunk, chunk, axis=1)
+
+    right = [(i, (i + 2) % dp) for i in range(dp)]
+    left = [(i, (i - 2) % dp) for i in range(dp)]
+    if rings == 4:
+        from_left = lax.ppermute(piece(zpos + 2), "dp", right)
+        from_right = lax.ppermute(piece(zpos - 1), "dp", left)
+        relayed = lax.ppermute(piece(zpos + 1) + from_left, "dp", right)
+        acc = piece(zpos) + from_right + relayed
+    else:
+        acc = piece(zpos - 1)
+        for step in range(rings - 1):
+            acc = lax.ppermute(acc, "dp", right) + piece(zpos - 2 - step)
     return (grad_hidden.astype(jnp.bfloat16), acc.astype(jnp.bfloat16))
 
 

time: 253 us -> 243 us (0.960)
  waiting for transfers between devices: 176 us -> 161 us
  other arithmetic: 4.09 us -> 14.3 us
  matrix products: 43.9 us -> 37.1 us
    ppermute x1, waiting for transfers between devices: 13.5 us -> 0.01 us  [on_device(): got = lax.ppermute(send, 'dp', [(i, i ^ 1) for i in range(dp)])]
    add x2, other arithmetic: 1.84 us -> 12.1 us  [the longest x1 11.1 us: on_device(): chip = keep + got]
    dot_general x1, matrix products: 10.9 us -> 7.28 us  [on_device(): lax.dot_general(grad_logits, columns_of(core), contract, preferred_elemen...]
    dot_general x1, matrix products: 13.6 us -> 10.5 us  [on_device(): jnp.dot(grad_logits, full_head, preferred_element_type=jnp.float32)]
  transfers between devices with their start and end apart: 6 -> 6, of which waited for: 5 -> 4; matrix products, arithmetic and copies ran while one was open for 9% -> 12% of each run, Pallas kernels for 0% -> 0%
where the time goes in v4:
time: 243 us
  waiting for transfers between devices  161 us (66%)
  matrix products  37.1 us (15%)
  other arithmetic  14.3 us (6%)
  between operations  14.3 us (6%)
  local copies, waits for them, and re-layouts  12.5 us (5%)
  starting transfers between devices  3.82 us (2%)
    reduce_scatter x1, waiting for transfers between devices, on_device(): part = lax.psum_scatter(chip, 'fsdp', scatter_dimension=0, tiled=True)  85.8 us
    all_gather x1, waiting for transfers between devices, on_device(): full_head = lax.all_gather(head, 'fsdp', axis=0, tiled=True)  65.6 us
    dot_general x1, matrix products, on_device(): lax.dot_general(hidden, full_head, (((1,), (1,)), ((), ())), preferred_el...  11.9 us
    add x1, other arithmetic, on_device(): chip = keep + got  11.1 us
    dot_general x1, matrix products, on_device(): jnp.dot(grad_logits, full_head, preferred_element_type=jnp.float32)  10.5 us
    dynamic_slice x1, local copies, waits for them, and re-layouts, columns_of(): lax.dynamic_slice_in_dim(hidden, (2 * j + parity) * chunk, chunk, axis=1)  8.91 us
    dot_general x1, matrix products, on_device(): lax.dot_general(grad_logits, columns_of(1 - core), contract, preferred_el...  7.41 us
    dot_general x1, matrix products, on_device(): lax.dot_general(grad_logits, columns_of(core), contract, preferred_elemen...  7.28 us
  transfers between devices with their start and end apart: 6, of which 4 were waited for; matrix products, arithmetic and copies ran while one was open for 12% of the time, Pallas kernels for 0%

profile of v4, /device:TPU:0, one launch (start us, length us, event | category | flops | bytes accessed | tf_op | source)
XLA Modules:
  0.0 242.8 jit_solution(8248656077541749130)
XLA Ops:
  7.2 0.0 all-gather.2.cloned.1.call-start
  7.2 0.7 all-gather.2.cloned.1.call-update
  7.9 0.0 reduce-scatter.2.cloned.1.call-start
  8.0 0.7 fusion.35
  8.7 0.1 copy.9
  8.8 8.9 %constant_dynamic-slice_fusion.5 = (bf16[768,1024]{1,0:T(8,128)(2,1)}, bf16[768,1024]{1,0:T(8,128)(2,1)}, bf16[768,1024]{1,0:T(8,128)(2,1)S(1)}, bf16[768,1024]{...) fusion(bf16[768,8192]{1,0:T(8,128)(2,1)} %param.6, ...), kind=kLoop, calls=%fused_computation.46 | loop fusion | bytes 25165856 | tf_op jit(solution)/shard_map/dynamic_slice | solution.py:34
  17.7 0.0 copy-start.6
  17.7 0.0 copy-start.7
  17.7 0.0 copy-start.8
  17.7 65.6 %all-gather.2.cloned.1.call-done = bf16[512,8192]{1,0:T(8,128)(2,1)} async-done(((bf16[32,8192]{1,0:T(8,128)(2,1)}), bf16[512,8192]{1,0:T(8,128)(2,1)}) %all-gather.2.cloned.1.call-update) | async-done | bytes 8388624 | tf_op jit(solution)/shard_map/all_gather | solution.py:23
  83.3 0.0 copy-start.2
  83.3 0.0 copy-start.3
  83.3 0.0 copy-start.4
  83.3 0.0 copy-start.5
  83.3 11.9 %fusion.41 = f32[768,512]{1,0:T(8,128)S(1)} fusion(bf16[768,8192]{1,0:T(8,128)(2,1)} %param.6, bf16[512,8192]{1,0:T(8,128)(2,1)} %all-gather.2.cloned.1.call-done), kind=kOutput, calls=%fused_computation.56 | convolution fusion | flops 6442450944 | bytes 22544384 | tf_op jit(solution)/shard_map/dot_general | solution.py:24
  95.3 2.4 broadcast_in_dim.5
  97.7 0.0 copy-done.6
  97.7 0.0 copy-done.7
  97.7 0.0 copy-done.8
  97.7 0.0 copy-done.2
  97.8 0.0 copy-done.3
  97.8 0.0 copy-done.4
  97.8 0.0 copy-done.5
  97.8 0.0 copy-start
  97.8 0.0 copy-start.1
  97.8 0.0 slice-start
  97.8 7.4 %fusion.8 = f32[512,4096]{1,0:T(8,128)} fusion(bf16[768,1024]{1,0:T(8,128)(2,1)S(1)} %copy-done.4, bf16[768,1024]{1,0:T(8,128)(2,1)S(1)} %copy-done.5, bf16[768,1024]{1,0:T(8,128)(2,1)S(1)} %copy-done.3, bf16[768,1024]{1,0:T(8,128)(2,1)S(1)} %copy-done.2, f32[768,512]{1,0:T(8,128)S(1)} %fusion.41, pred[96,8,4,128]{3,2,1,0:T(4,128)(4,1)S(1)} %bitcast.18, ...), kind=kOutput, calls=%fused_computation.8 | convolution fusion | flops 3249143808 | bytes 16655360 | tf_op jit(solution)/shard_map/dot_general | solution.py:40
  105.2 0.0 collective-permute-start
  105.2 0.0 slice-start.1
  105.2 0.0 copy-done
  105.2 0.0 copy-done.1
  105.2 7.3 %fusion = f32[512,4096]{1,0:T(8,128)} fusion(bf16[768,1024]{1,0:T(8,128)(2,1)S(1)} %get-tuple-element.8, bf16[768,1024]{1,0:T(8,128)(2,1)S(1)} %get-tuple-element.9, bf16[768,1024]{1,0:T(8,128)(2,1)S(1)} %copy-done, bf16[768,1024]{1,0:T(8,128)(2,1)S(1)} %copy-done.1, f32[768,512]{1,0:T(8,128)S(1)} %fusion.41, pred[96,8,4,128]{3,2,1,0:T(4,128)(4,1)S(1)} %bitcast.19, ...), kind=kOutput, calls=%fused_computation | convolution fusion | flops 3249143808 | bytes 16655360 | tf_op jit(solution)/shard_map/dot_general | solution.py:44
  112.5 0.0 slice-done
  112.5 0.0 slice-done.1
  112.5 10.5 %fusion.16 = bf16[768,8192]{1,0:T(8,128)(2,1)} fusion(bf16[512,8192]{1,0:T(8,128)(2,1)S(1)} %bitcast.23, f32[768,512]{1,0:T(8,128)S(1)} %fusion.41, pred[96,8,4,128]{3,2,1,0:T(4,128)(4,1)S(1)} %bitcast.20, s32[768]{0:T(1024)S(1)} %copy-done.6, f32[768]{0:T(1024)S(1)} %copy-done.7, f32[768]{0:T(1024)S(1)} %copy-done.8), kind=kOutput, calls=%fused_computation.18 | convolution fusion | flops 6445203456 | bytes 22946816 | tf_op jit(solution)/shard_map/dot_general | solution.py:47
  123.0 0.0 collective-permute-done
  123.0 11.1 %add.110 = f32[512,4096]{1,0:T(8,128)} add(f32[512,4096]{1,0:T(8,128)} %fusion, f32[512,4096]{1,0:T(8,128)} %collective-permute-done) | non-fusion elementwise | flops 2097152 | bytes 25165824 | tf_op jit(solution)/shard_map/add | solution.py:49
  134.2 0.0 reduce-scatter.2.cloned.1.call-update
  134.2 85.8 %reduce-scatter.2.cloned.1.call-done = f32[32,4096]{1,0:T(8,128)} async-done(((f32[512,4096]{1,0:T(8,128)}), f32[32,4096]{1,0:T(8,128)}) %reduce-scatter.2.cloned.1.call-update) | async-done | bytes 524304 | tf_op jit(solution)/shard_map/reduce_scatter | solution.py:50
  220.0 1.0 constant_dynamic-slice_fusion.1
  221.0 1.6 collective-permute-start.2
  222.7 1.7 collective-permute-start.1
  224.3 2.9 %collective-permute-done.2 = f32[32,1024]{1,0:T(8,128)S(1)} collective-permute-done((f32[32,1024]{1,0:T(8,128)S(1)}, f32[32,1024]{1,0:T(8,128)S(1)}, u32[]{:S(2)}, u32[]{:S(2)}) %collective-permute-start.2) | collective-permute-done | bytes 131104 | tf_op jit(solution)/shard_map/ppermute | solution.py:57
  227.3 0.9 dynamic-slice_add_fusion
  228.2 0.4 collective-permute-start.3
  228.6 0.0 collective-permute-done.1
  228.6 5.8 %collective-permute-done.3 = f32[32,1024]{1,0:T(8,128)S(1)} collective-permute-done((f32[32,1024]{1,0:T(8,128)S(1)}, f32[32,1024]{1,0:T(8,128)S(1)}, u32[]{:S(2)}, u32[]{:S(2)}) %collective-permute-start.3) | collective-permute-done | bytes 131104 | tf_op jit(solution)/shard_map/ppermute | solution.py:59
  234.4 1.6 add_convert_fusion
  (2 shorter events, 0.0 us)
Async XLA Ops:
  7.2 76.1 %all-gather.2.cloned.1.call-start = ((), (), s32[]{:S(2)}) async-start(), calls=%async_computation.1 | async-start | bytes 8912896 | tf_op jit(solution)/shard_map/all_gather | solution.py:23
  7.9 212.1 %reduce-scatter.2.cloned.1.call-start = ((), (), s32[]{:S(2)}) async-start(), calls=%async_computation.2 | async-start | bytes 8912896 | tf_op jit(solution)/shard_map/reduce_scatter | solution.py:50
  17.7 80.0 %copy-start.6 = (s32[768]{0:T(1024)S(1)}, s32[768]{0:T(1024)}, u32[]{:S(2)}) copy-start(s32[768]{0:T(1024)} %param.8) | copy-start | bytes 9220
  17.7 80.0 %copy-start.7 = (f32[768]{0:T(1024)S(1)}, f32[768]{0:T(1024)}, u32[]{:S(2)}) copy-start(f32[768]{0:T(1024)} %param.9) | copy-start | bytes 9220
  17.7 80.0 %copy-start.8 = (f32[768]{0:T(1024)S(1)}, f32[768]{0:T(1024)}, u32[]{:S(2)}) copy-start(f32[768]{0:T(1024)} %param.10) | copy-start | bytes 9220
  83.3 14.5 %copy-start.2 = (bf16[768,1024]{1,0:T(8,128)(2,1)S(1)}, bf16[768,1024]{1,0:T(8,128)(2,1)}, u32[]{:S(2)}) copy-start(bf16[768,1024]{1,0:T(8,128)(2,1)} %get-tuple-element.6) | copy-start | bytes 4718596
  83.3 14.5 %copy-start.3 = (bf16[768,1024]{1,0:T(8,128)(2,1)S(1)}, bf16[768,1024]{1,0:T(8,128)(2,1)}, u32[]{:S(2)}) copy-start(bf16[768,1024]{1,0:T(8,128)(2,1)} %get-tuple-element.7) | copy-start | bytes 4718596
  83.3 14.5 %copy-start.4 = (bf16[768,1024]{1,0:T(8,128)(2,1)S(1)}, bf16[768,1024]{1,0:T(8,128)(2,1)}, u32[]{:S(2)}) copy-start(bf16[768,1024]{1,0:T(8,128)(2,1)} %get-tuple-element.12) | copy-start | bytes 4718596
  83.3 14.5 %copy-start.5 = (bf16[768,1024]{1,0:T(8,128)(2,1)S(1)}, bf16[768,1024]{1,0:T(8,128)(2,1)}, u32[]{:S(2)}) copy-start(bf16[768,1024]{1,0:T(8,128)(2,1)} %get-tuple-element.13) | copy-start | bytes 4718596
  97.8 7.4 %copy-start = (bf16[768,1024]{1,0:T(8,128)(2,1)S(1)}, bf16[768,1024]{1,0:T(8,128)(2,1)}, u32[]{:S(2)}) copy-start(bf16[768,1024]{1,0:T(8,128)(2,1)} %get-tuple-element.10) | copy-start | bytes 4718596
  97.8 7.4 %copy-start.1 = (bf16[768,1024]{1,0:T(8,128)(2,1)S(1)}, bf16[768,1024]{1,0:T(8,128)(2,1)}, u32[]{:S(2)}) copy-start(bf16[768,1024]{1,0:T(8,128)(2,1)} %get-tuple-element.11) | copy-start | bytes 4718596
  97.8 14.7 %slice-start = ((s8[8388608]{0:T(1024)(128)(4,1)}), s8[4194304]{0:T(1024)(128)(4,1)S(1)}, s32[]{:S(2)}) async-start(s8[8388608]{0:T(1024)(128)(4,1)} %bitcast.22), calls=%async_computation.3 | async-start | bytes 8388608
  105.2 17.8 %collective-permute-start = (f32[512,4096]{1,0:T(8,128)}, f32[512,4096]{1,0:T(8,128)}, u32[]{:S(2)}, u32[]{:S(2)}) collective-permute-start(f32[512,4096]{1,0:T(8,128)} %fusion.8), channel_id=1, source_target_pairs={{0,16},{16,0},{32,48},{48,32},{64,80},{80,64},{96,112},{112,96},{1... | collective-permute-start | bytes 25165832 | tf_op jit(solution)/shard_map/ppermute | solution.py:43
  105.2 7.3 %slice-start.1 = ((s8[8388608]{0:T(1024)(128)(4,1)}), s8[4194304]{0:T(1024)(128)(4,1)S(1)}, s32[]{:S(2)}) async-start(s8[8388608]{0:T(1024)(128)(4,1)} %bitcast.22), calls=%async_computation.4 | async-start | bytes 8388608
  221.0 6.2 %collective-permute-start.2 = (f32[32,1024]{1,0:T(8,128)S(1)}, f32[32,1024]{1,0:T(8,128)S(1)}, u32[]{:S(2)}, u32[]{:S(2)}) collective-permute-start(f32[32,1024]{1,0:T(8,128)S(1)} %get-tuple-element.15), channel_id=1, source_target_pairs={{0,32},{16,48},{32,64},{48,80},{64,96},{80,112},{96,0},{112,16},{1... | collective-permute-start | bytes 393224 | tf_op jit(solution)/shard_map/ppermute | solution.py:57
  222.7 6.0 %collective-permute-start.1 = (f32[32,1024]{1,0:T(8,128)S(1)}, f32[32,1024]{1,0:T(8,128)S(1)}, u32[]{:S(2)}, u32[]{:S(2)}) collective-permute-start(f32[32,1024]{1,0:T(8,128)S(1)} %get-tuple-element.14), channel_id=1, source_target_pairs={{0,96},{16,112},{32,0},{48,16},{64,32},{80,48},{96,64},{112,80},{1... | collective-permute-start | bytes 393224 | tf_op jit(solution)/shard_map/ppermute | solution.py:58
  228.2 6.2 %collective-permute-start.3 = (f32[32,1024]{1,0:T(8,128)S(1)}, f32[32,1024]{1,0:T(8,128)S(1)}, u32[]{:S(2)}, u32[]{:S(2)}) collective-permute-start(f32[32,1024]{1,0:T(8,128)S(1)} %dynamic-slice_add_fusion), channel_id=1, source_target_pairs={{0,32},{16,48},{32,64},{48,80},{64,96},{80,112},{96,0},{112,16},{1... | collective-permute-start | bytes 393224 | tf_op jit(solution)/shard_map/ppermute | solution.py:59
Sparse Core Ops, SparseCore 0:
  10.1 73.1 all-gather.1
  134.3 85.6 reduce-scatter.1

commit v5 on v4

--- a/solution.py
+++ b/solution.py
@@ -41,11 +41,11 @@
         grad_logits, columns_of(1 - core), contract, preferred_element_type=jnp.float32
     )
     got = lax.ppermute(send, "dp", [(i, i ^ 1) for i in range(dp)])
+    grad_hidden = jnp.dot(grad_logits, full_head, preferred_element_type=jnp.float32)
+    got, grad_hidden, late_logits = lax.optimization_barrier((got, grad_hidden, grad_logits))
     keep = lax.dot_general(
-        grad_logits, columns_of(core), contract, preferred_element_type=jnp.float32
+        late_logits, columns_of(core), contract, preferred_element_type=jnp.float32
     )
-    grad_hidden = jnp.dot(grad_logits, full_head, preferred_element_type=jnp.float32)
-    keep, grad_hidden = lax.optimization_barrier((keep, grad_hidden))
     chip = keep + got
     part = lax.psum_scatter(chip, "fsdp", scatter_dimension=0, tiled=True)
     def piece(k):

time: 243 us -> 240 us (0.988)
  other arithmetic: 14.3 us -> 3.17 us
  matrix products: 37.1 us -> 43.9 us
    add x1 -> x0, other arithmetic: 11.1 us -> none  [on_device(): chip = keep + got]
    dot_general x1, matrix products: 10.5 us -> 13.9 us  [on_device(): jnp.dot(grad_logits, full_head, preferred_element_type=jnp.float32)]
  transfers between devices with their start and end apart: 6 -> 6, of which waited for: 4 -> 4; matrix products, arithmetic and copies ran while one was open for 12% -> 10% of each run, Pallas kernels for 0% -> 0%
where the time goes in v5:
time: 240 us
  waiting for transfers between devices  161 us (67%)
  matrix products  43.9 us (18%)
  between operations  14.2 us (6%)
  local copies, waits for them, and re-layouts  13.7 us (6%)
  starting transfers between devices  3.79 us (2%)
  other arithmetic  3.17 us (1%)
    reduce_scatter x1, waiting for transfers between devices, on_device(): part = lax.psum_scatter(chip, 'fsdp', scatter_dimension=0, tiled=True)  85.8 us
    all_gather x1, waiting for transfers between devices, on_device(): full_head = lax.all_gather(head, 'fsdp', axis=0, tiled=True)  65.5 us
    dot_general x1, matrix products, on_device(): jnp.dot(grad_logits, full_head, preferred_element_type=jnp.float32)  13.9 us
    dot_general x1, matrix products, on_device(): lax.dot_general(hidden, full_head, (((1,), (1,)), ((), ())), preferred_el...  13.4 us
    dot_general x1, matrix products, on_device(): lax.dot_general(late_logits, columns_of(core), contract, preferred_elemen...  9.42 us
    dynamic_slice x1, local copies, waits for them, and re-layouts, columns_of(): lax.dynamic_slice_in_dim(hidden, (2 * j + parity) * chunk, chunk, axis=1)  8.98 us
    dot_general x1, matrix products, on_device(): lax.dot_general(grad_logits, columns_of(1 - core), contract, preferred_el...  7.17 us
    ppermute x1, waiting for transfers between devices, on_device(): relayed = lax.ppermute(piece(zpos + 1) + from_left, 'dp', right)  5.84 us
  transfers between devices with their start and end apart: 6, of which 4 were waited for; matrix products, arithmetic and copies ran while one was open for 10% of the time, Pallas kernels for 0%

profile of v5, /device:TPU:0, one launch (start us, length us, event | category | flops | bytes accessed | tf_op | source)
XLA Modules:
  0.0 239.6 jit_solution(15418789582610294629)
XLA Ops:
  7.2 0.0 all-gather.2.cloned.1.call-start
  7.2 0.7 all-gather.2.cloned.1.call-update
  7.9 0.0 reduce-scatter.2.cloned.1.call-start
  8.0 0.7 fusion.32
  8.7 0.1 copy.9
  8.8 0.0 copy-start.6
  8.8 0.0 copy-start.7
  8.8 0.0 copy-start.8
  8.8 9.0 %constant_dynamic-slice_fusion.5 = (bf16[768,1024]{1,0:T(8,128)(2,1)S(1)}, bf16[768,1024]{1,0:T(8,128)(2,1)S(1)}, bf16[768,1024]{1,0:T(8,128)(2,1)}, bf16[768,10...) fusion(bf16[768,8192]{1,0:T(8,128)(2,1)} %param.6, ...), kind=kLoop, calls=%fused_computation.41 | loop fusion | bytes 25165856 | tf_op jit(solution)/shard_map/dynamic_slice | solution.py:34
  17.8 65.5 %all-gather.2.cloned.1.call-done = bf16[512,8192]{1,0:T(8,128)(2,1)} async-done(((bf16[32,8192]{1,0:T(8,128)(2,1)}), bf16[512,8192]{1,0:T(8,128)(2,1)}) %all-gather.2.cloned.1.call-update) | async-done | bytes 8388624 | tf_op jit(solution)/shard_map/all_gather | solution.py:23
  83.3 2.4 %broadcast_in_dim.5 = pred[768,4,128]{2,1,0:T(4,128)(4,1)S(1)} broadcast(pred[768,4]{1,0:T(8,128)(4,1)S(1)} %bitcast.19), dimensions={0,1} | broadcast | bytes 396288 | tf_op jit(solution)/shard_map/broadcast_in_dim | solution.py:22
  85.8 0.0 copy-done.6
  85.8 0.0 copy-done.7
  85.8 0.0 copy-done.8
  85.8 0.0 copy-start.2
  85.8 0.0 copy-start.3
  85.8 0.0 copy-start.4
  85.8 0.0 copy-start.5
  85.8 13.4 %multiply_convert_fusion = (bf16[768,512]{1,0:T(8,128)(2,1)}, f32[768,512]{1,0:T(8,128)S(1)}) fusion(pred[96,8,4,128]{3,2,1,0:T(4,128)(4,1)S(1)} %bitcast.16, s32[768]{0:T(1024)S(1)} %copy-done.6, f32[768]{0:T(1024)S(1)} %copy-done.7, f32[768]{0:T(1024)S(1)} %copy-done.8, bf16[768,8192]{1,0:T(8,128)(2,1)} %param.6, ...), kind=kOutput, calls=%fused_computation.17 | convolution fusion | flops 6445203456 | bytes 23733248 | tf_op jit(solution)/shard_map/dot_general | solution.py:24
  99.2 0.0 copy-start.9
  99.2 1.2 copy-done.9
  100.4 0.0 copy-done.2
  100.4 0.0 copy-done.3
  100.4 0.0 copy-done.4
  100.4 0.0 copy-done.5
  100.4 7.2 %fusion = f32[512,4096]{1,0:T(8,128)} fusion(bf16[768,1024]{1,0:T(8,128)(2,1)S(1)} %copy-done.2, bf16[768,1024]{1,0:T(8,128)(2,1)S(1)} %copy-done.3, bf16[768,1024]{1,0:T(8,128)(2,1)S(1)} %copy-done.4, bf16[768,1024]{1,0:T(8,128)(2,1)S(1)} %copy-done.5, f32[768,512]{1,0:T(8,128)S(1)} %get-tuple-element.19, pred[96,8,4,128]{3,2,1,0:T(4,128)(4,1)S(1)} %bitcast.17, ...), kind=kOutput, calls=%fused_computation | convolution fusion | flops 3249143808 | bytes 16655360 | tf_op jit(solution)/shard_map/dot_general | solution.py:40
  107.6 0.0 copy-start
  107.6 0.0 copy-start.1
  107.6 0.0 collective-permute-start
  107.6 13.9 %fusion.19 = bf16[768,8192]{1,0:T(8,128)(2,1)} fusion(bf16[512,8192]{1,0:T(8,128)(2,1)} %all-gather.2.cloned.1.call-done, f32[768,512]{1,0:T(8,128)} %copy-done.9, pred[96,8,4,128]{3,2,1,0:T(4,128)(4,1)S(1)} %bitcast.18, s32[768]{0:T(1024)S(1)} %copy-done.6, f32[768]{0:T(1024)S(1)} %copy-done.7, f32[768]{0:T(1024)S(1)} %copy-done.8), kind=kOutput, calls=%fused_computation.19 | convolution fusion | flops 6445203456 | bytes 22946816 | tf_op jit(solution)/shard_map/dot_general | solution.py:44
  121.5 0.0 collective-permute-done
  121.5 0.0 copy-done
  121.5 0.0 copy-done.1
  121.5 9.4 %fusion.10 = f32[512,4096]{1,0:T(8,128)} fusion(f32[512,4096]{1,0:T(8,128)S(1)} %collective-permute-done, bf16[768,512]{1,0:T(8,128)(2,1)} %get-tuple-element.6, bf16[768,1024]{1,0:T(8,128)(2,1)S(1)} %copy-done, bf16[768,1024]{1,0:T(8,128)(2,1)S(1)} %copy-done.1, bf16[768,1024]{1,0:T(8,128)(2,1)S(1)} %get-tuple-element.9, ...), kind=kOutput, calls=%fused_computation.10 | convolution fusion | flops 3248488448 | bytes 23855104 | tf_op jit(solution)/shard_map/dot_general | solution.py:46
  130.9 0.0 reduce-scatter.2.cloned.1.call-update
  131.0 85.8 %reduce-scatter.2.cloned.1.call-done = f32[32,4096]{1,0:T(8,128)} async-done(((f32[512,4096]{1,0:T(8,128)}), f32[32,4096]{1,0:T(8,128)}) %reduce-scatter.2.cloned.1.call-update) | async-done | bytes 524304 | tf_op jit(solution)/shard_map/reduce_scatter | solution.py:50
  216.8 1.0 constant_dynamic-slice_fusion.1
  217.8 1.6 collective-permute-start.2
  219.4 1.7 collective-permute-start.1
  221.1 2.9 %collective-permute-done.2 = f32[32,1024]{1,0:T(8,128)S(1)} collective-permute-done((f32[32,1024]{1,0:T(8,128)S(1)}, f32[32,1024]{1,0:T(8,128)S(1)}, u32[]{:S(2)}, u32[]{:S(2)}) %collective-permute-start.2) | collective-permute-done | bytes 131104 | tf_op jit(solution)/shard_map/ppermute | solution.py:57
  224.1 0.9 dynamic-slice_add_fusion
  225.0 0.4 collective-permute-start.3
  225.4 0.0 collective-permute-done.1
  225.4 5.8 %collective-permute-done.3 = f32[32,1024]{1,0:T(8,128)S(1)} collective-permute-done((f32[32,1024]{1,0:T(8,128)S(1)}, f32[32,1024]{1,0:T(8,128)S(1)}, u32[]{:S(2)}, u32[]{:S(2)}) %collective-permute-start.3) | collective-permute-done | bytes 131104 | tf_op jit(solution)/shard_map/ppermute | solution.py:59
  231.2 1.6 add_convert_fusion
  (1 shorter events, 0.0 us)
Async XLA Ops:
  7.2 76.1 %all-gather.2.cloned.1.call-start = ((), (), s32[]{:S(2)}) async-start(), calls=%async_computation.1 | async-start | bytes 8912896 | tf_op jit(solution)/shard_map/all_gather | solution.py:23
  7.9 208.9 %reduce-scatter.2.cloned.1.call-start = ((), (), s32[]{:S(2)}) async-start(), calls=%async_computation.2 | async-start | bytes 8912896 | tf_op jit(solution)/shard_map/reduce_scatter | solution.py:50
  8.8 77.0 %copy-start.6 = (s32[768]{0:T(1024)S(1)}, s32[768]{0:T(1024)}, u32[]{:S(2)}) copy-start(s32[768]{0:T(1024)} %param.8) | copy-start | bytes 9220
  8.8 77.0 %copy-start.7 = (f32[768]{0:T(1024)S(1)}, f32[768]{0:T(1024)}, u32[]{:S(2)}) copy-start(f32[768]{0:T(1024)} %param.9) | copy-start | bytes 9220
  8.8 77.0 %copy-start.8 = (f32[768]{0:T(1024)S(1)}, f32[768]{0:T(1024)}, u32[]{:S(2)}) copy-start(f32[768]{0:T(1024)} %param.10) | copy-start | bytes 9220
  85.8 14.6 %copy-start.2 = (bf16[768,1024]{1,0:T(8,128)(2,1)S(1)}, bf16[768,1024]{1,0:T(8,128)(2,1)}, u32[]{:S(2)}) copy-start(bf16[768,1024]{1,0:T(8,128)(2,1)} %get-tuple-element.10) | copy-start | bytes 4718596
  85.8 14.6 %copy-start.3 = (bf16[768,1024]{1,0:T(8,128)(2,1)S(1)}, bf16[768,1024]{1,0:T(8,128)(2,1)}, u32[]{:S(2)}) copy-start(bf16[768,1024]{1,0:T(8,128)(2,1)} %get-tuple-element.11) | copy-start | bytes 4718596
  85.8 14.6 %copy-start.4 = (bf16[768,1024]{1,0:T(8,128)(2,1)S(1)}, bf16[768,1024]{1,0:T(8,128)(2,1)}, u32[]{:S(2)}) copy-start(bf16[768,1024]{1,0:T(8,128)(2,1)} %get-tuple-element.12) | copy-start | bytes 4718596
  85.8 14.6 %copy-start.5 = (bf16[768,1024]{1,0:T(8,128)(2,1)S(1)}, bf16[768,1024]{1,0:T(8,128)(2,1)}, u32[]{:S(2)}) copy-start(bf16[768,1024]{1,0:T(8,128)(2,1)} %get-tuple-element.13) | copy-start | bytes 4718596
  99.2 1.2 copy-start.9
  107.6 13.9 %copy-start = (bf16[768,1024]{1,0:T(8,128)(2,1)S(1)}, bf16[768,1024]{1,0:T(8,128)(2,1)}, u32[]{:S(2)}) copy-start(bf16[768,1024]{1,0:T(8,128)(2,1)} %get-tuple-element.14) | copy-start | bytes 4718596
  107.6 13.9 %copy-start.1 = (bf16[768,1024]{1,0:T(8,128)(2,1)S(1)}, bf16[768,1024]{1,0:T(8,128)(2,1)}, u32[]{:S(2)}) copy-start(bf16[768,1024]{1,0:T(8,128)(2,1)} %get-tuple-element.15) | copy-start | bytes 4718596
  107.6 13.9 %collective-permute-start = (f32[512,4096]{1,0:T(8,128)}, f32[512,4096]{1,0:T(8,128)S(1)}, u32[]{:S(2)}, u32[]{:S(2)}) collective-permute-start(f32[512,4096]{1,0:T(8,128)} %fusion), channel_id=1, source_target_pairs={{0,16},{16,0},{32,48},{48,32},{64,80},{80,64},{96,112},{112,96},{1... | collective-permute-start | bytes 25165832 | tf_op jit(solution)/shard_map/ppermute | solution.py:43
  217.8 6.2 %collective-permute-start.2 = (f32[32,1024]{1,0:T(8,128)S(1)}, f32[32,1024]{1,0:T(8,128)S(1)}, u32[]{:S(2)}, u32[]{:S(2)}) collective-permute-start(f32[32,1024]{1,0:T(8,128)S(1)} %get-tuple-element.17), channel_id=1, source_target_pairs={{0,32},{16,48},{32,64},{48,80},{64,96},{80,112},{96,0},{112,16},{1... | collective-permute-start | bytes 393224 | tf_op jit(solution)/shard_map/ppermute | solution.py:57
  219.4 6.0 %collective-permute-start.1 = (f32[32,1024]{1,0:T(8,128)S(1)}, f32[32,1024]{1,0:T(8,128)S(1)}, u32[]{:S(2)}, u32[]{:S(2)}) collective-permute-start(f32[32,1024]{1,0:T(8,128)S(1)} %get-tuple-element.16), channel_id=1, source_target_pairs={{0,96},{16,112},{32,0},{48,16},{64,32},{80,48},{96,64},{112,80},{1... | collective-permute-start | bytes 393224 | tf_op jit(solution)/shard_map/ppermute | solution.py:58
  225.0 6.2 %collective-permute-start.3 = (f32[32,1024]{1,0:T(8,128)S(1)}, f32[32,1024]{1,0:T(8,128)S(1)}, u32[]{:S(2)}, u32[]{:S(2)}) collective-permute-start(f32[32,1024]{1,0:T(8,128)S(1)} %dynamic-slice_add_fusion), channel_id=1, source_target_pairs={{0,32},{16,48},{32,64},{48,80},{64,96},{80,112},{96,0},{112,16},{1... | collective-permute-start | bytes 393224 | tf_op jit(solution)/shard_map/ppermute | solution.py:59
Sparse Core Ops, SparseCore 0:
  10.1 73.1 all-gather.1
  131.1 85.7 reduce-scatter.1

commit v6 on v5

--- a/solution.py
+++ b/solution.py
@@ -47,7 +47,10 @@
         late_logits, columns_of(core), contract, preferred_element_type=jnp.float32
     )
     chip = keep + got
-    part = lax.psum_scatter(chip, "fsdp", scatter_dimension=0, tiled=True)
+    if lax.axis_size("fsdp") == 16:
+        part = plane_scatter(chip)
+    else:
+        part = lax.psum_scatter(chip, "fsdp", scatter_dimension=0, tiled=True)
     def piece(k):
         return lax.dynamic_slice_in_dim(part, (k % rings) * chunk, chunk, axis=1)
 
@@ -65,6 +68,41 @@
     return (grad_hidden.astype(jnp.bfloat16), acc.astype(jnp.bfloat16))
 
 
+def ring_scatter(blocks, pos, ahead, behind):
+    from_behind = lax.ppermute(blocks(pos + 2), "fsdp", ahead)
+    from_ahead = lax.ppermute(blocks(pos - 1), "fsdp", behind)
+    relayed = lax.ppermute(blocks(pos + 1) + from_behind, "fsdp", ahead)
+    return blocks(pos) + from_ahead + relayed
+
+
+def mirrored_scatter(blocks, pos, ahead, behind):
+    return ring_scatter(lambda k: blocks(-k), -pos, behind, ahead)
+
+
+def plane_scatter(chip):
+    f = lax.axis_index("fsdp")
+    xi, yi = f // 4, f % 4
+    x_up = [(i, (i + 4) % 16) for i in range(16)]
+    x_down = [(i, (i - 4) % 16) for i in range(16)]
+    y_up = [(i, 4 * (i // 4) + (i + 1) % 4) for i in range(16)]
+    y_down = [(i, 4 * (i // 4) + (i - 1) % 4) for i in range(16)]
+    rows, width = chip.shape
+    quarter = width // 4
+    grid = chip.reshape(4, 4, rows // 16, width)
+    outs = []
+    for q in range(4):
+        data = grid[:, :, :, q * quarter:(q + 1) * quarter]
+        scatter = ring_scatter if q % 2 == 0 else mirrored_scatter
+        if q < 2:
+            first = scatter(lambda k: lax.dynamic_index_in_dim(data, k % 4, 0, False), xi, x_up, x_down)
+            done = scatter(lambda k: lax.dynamic_index_in_dim(first, k % 4, 0, False), yi, y_up, y_down)
+        else:
+            first = scatter(lambda k: lax.dynamic_index_in_dim(data, k % 4, 1, False), yi, y_up, y_down)
+            done = scatter(lambda k: lax.dynamic_index_in_dim(first, k % 4, 0, False), xi, x_up, x_down)
+        outs.append(done)
+    return jnp.concatenate(outs, axis=1)
+
+
 def solution(mesh):
     return jax.shard_map(
         on_device,

time: 240 us -> 241 us (level)
  waiting for transfers between devices: 161 us -> 135 us
  starting transfers between devices: 3.79 us -> 28.5 us
  local copies, waits for them, and re-layouts: 13.7 us -> 18.7 us
    reduce_scatter x1 -> x0, waiting for transfers between devices: 85.8 us -> none  [on_device(): part = lax.psum_scatter(chip, 'fsdp', scatter_dimension=0, tiled=True)]
    ppermute x0 -> x24, waiting for transfers between devices: none -> 59.8 us  [the longest x8 30.5 us: ring_scatter(): relayed = lax.ppermute(blocks(pos + 1) + from_behind, 'fsdp', ahead)]
    ppermute x0 -> x24, starting transfers between devices: none -> 24.7 us  [the longest x8 9.01 us: ring_scatter(): from_behind = lax.ppermute(blocks(pos + 2), 'fsdp', ahead)]
    slice x0 -> x1, local copies, waits for them, and re-layouts: none -> 3.05 us  [plane_scatter(): data = grid[:, :, :, q * quarter:(q + 1) * quarter]]
    squeeze x0 -> x8, local copies, waits for them, and re-layouts: none -> 2.49 us  [the longest x2 1.4 us: plane_scatter(): lax.dynamic_index_in_dim(data, k % 4, 1, False)]
  transfers between devices with their start and end apart: 6 -> 29, of which waited for: 4 -> 15; matrix products, arithmetic and copies ran while one was open for 10% -> 11% of each run, Pallas kernels for 0% -> 0%
where the time goes in v6:
time: 241 us
  waiting for transfers between devices  135 us (56%)
  matrix products  42.3 us (18%)
  starting transfers between devices  28.5 us (12%)
  local copies, waits for them, and re-layouts  18.7 us (8%)
  between operations  14.5 us (6%)
    all_gather x1, waiting for transfers between devices, on_device(): full_head = lax.all_gather(head, 'fsdp', axis=0, tiled=True)  65.4 us
    ppermute x8, waiting for transfers between devices, ring_scatter(): relayed = lax.ppermute(blocks(pos + 1) + from_behind, 'fsdp', ahead)  30.5 us
    ppermute x8, waiting for transfers between devices, ring_scatter(): from_behind = lax.ppermute(blocks(pos + 2), 'fsdp', ahead)  29.3 us
    dot_general x1, matrix products, on_device(): jnp.dot(grad_logits, full_head, preferred_element_type=jnp.float32)  13.9 us
    dot_general x1, matrix products, on_device(): lax.dot_general(hidden, full_head, (((1,), (1,)), ((), ())), preferred_el...  12.3 us
    dynamic_slice x1, local copies, waits for them, and re-layouts, columns_of(): lax.dynamic_slice_in_dim(hidden, (2 * j + parity) * chunk, chunk, axis=1)  9.16 us
    ppermute x8, starting transfers between devices, ring_scatter(): from_behind = lax.ppermute(blocks(pos + 2), 'fsdp', ahead)  9.01 us
    dot_general x1, matrix products, on_device(): lax.dot_general(late_logits, columns_of(core), contract, preferred_elemen...  8.85 us
  transfers between devices with their start and end apart: 29, of which 15 were waited for; matrix products, arithmetic and copies ran while one was open for 11% of the time, Pallas kernels for 0%

profile of v6, /device:TPU:0, one launch (start us, length us, event | category | flops | bytes accessed | tf_op | source)
XLA Modules:
  0.0 240.9 jit_solution(6820461444946639587)
XLA Ops:
  7.2 0.7 all-gather.2.cloned.1.call-update
  7.9 0.7 fusion.40
  8.7 9.2 %constant_dynamic-slice_fusion.5 = (bf16[768,1024]{1,0:T(8,128)(2,1)S(1)}, bf16[768,1024]{1,0:T(8,128)(2,1)}, bf16[768,1024]{1,0:T(8,128)(2,1)}, bf16[768,1024]{...) fusion(bf16[768,8192]{1,0:T(8,128)(2,1)} %param.6, ...), kind=kLoop, calls=%fused_computation.80 | loop fusion | bytes 25165856 | tf_op jit(solution)/shard_map/dynamic_slice | solution.py:34
  17.9 65.4 %all-gather.2.cloned.1.call-done = bf16[512,8192]{1,0:T(8,128)(2,1)} async-done(((bf16[32,8192]{1,0:T(8,128)(2,1)}), bf16[512,8192]{1,0:T(8,128)(2,1)}) %all-gather.2.cloned.1.call-update) | async-done | bytes 8388624 | tf_op jit(solution)/shard_map/all_gather | solution.py:23
  83.3 2.4 %broadcast_in_dim.5 = pred[768,4,128]{2,1,0:T(4,128)(4,1)S(1)} broadcast(pred[768,4]{1,0:T(8,128)(4,1)S(1)} %bitcast.101), dimensions={0,1} | broadcast | bytes 396288 | tf_op jit(solution)/shard_map/broadcast_in_dim | solution.py:22
  85.8 12.3 %multiply_convert_fusion = (bf16[768,512]{1,0:T(8,128)(2,1)S(1)}, f32[768,512]{1,0:T(8,128)S(1)}) fusion(pred[96,8,4,128]{3,2,1,0:T(4,128)(4,1)S(1)} %bitcast.98, s32[768]{0:T(1024)S(1)} %copy-done.11, f32[768]{0:T(1024)S(1)} %copy-done.12, f32[768]{0:T(1024)S(1)} %copy-done.13, bf16[768,8192]{1,0:T(8,128)(2,1)} %param.6, ...), kind=kOutput, calls=%fused_computation.17 | convolution fusion | flops 6445203456 | bytes 23733248 | tf_op jit(solution)/shard_map/dot_general | solution.py:24
  98.2 7.2 %fusion = f32[512,4096]{1,0:T(8,128)} fusion(bf16[768,1024]{1,0:T(8,128)(2,1)S(1)} %copy-done.7, bf16[768,1024]{1,0:T(8,128)(2,1)S(1)} %copy-done.8, bf16[768,1024]{1,0:T(8,128)(2,1)S(1)} %copy-done.9, bf16[768,1024]{1,0:T(8,128)(2,1)S(1)} %copy-done.10, f32[768,512]{1,0:T(8,128)S(1)} %get-tuple-element.39, pred[96,8,4,128]{3,2,1,0:T(4,128)(4,1)S(1)} %bitcast.99, ...), kind=kOutput, calls=%fused_computation | convolution fusion | flops 3249143808 | bytes 16655360 | tf_op jit(solution)/shard_map/dot_general | solution.py:40
  105.5 13.9 %fusion.19 = bf16[768,8192]{1,0:T(8,128)(2,1)} fusion(bf16[512,8192]{1,0:T(8,128)(2,1)} %all-gather.2.cloned.1.call-done, f32[768,512]{1,0:T(8,128)} %copy-done.14, pred[96,8,4,128]{3,2,1,0:T(4,128)(4,1)S(1)} %bitcast.100, s32[768]{0:T(1024)S(1)} %copy-done.11, f32[768]{0:T(1024)S(1)} %copy-done.12, f32[768]{0:T(1024)S(1)} %copy-done.13), kind=kOutput, calls=%fused_computation.19 | convolution fusion | flops 6445203456 | bytes 22946816 | tf_op jit(solution)/shard_map/dot_general | solution.py:44
  119.4 8.8 %fusion.10 = f32[512,4096]{1,0:T(8,128)S(1)} fusion(f32[512,4096]{1,0:T(8,128)} %collective-permute-done, bf16[768,512]{1,0:T(8,128)(2,1)S(1)} %get-tuple-element.6, bf16[768,1024]{1,0:T(8,128)(2,1)S(1)} %copy-done.5, bf16[768,1024]{1,0:T(8,128)(2,1)S(1)} %copy-done.6, bf16[768,1024]{1,0:T(8,128)(2,1)S(1)} %copy-done.4, ...), kind=kOutput, calls=%fused_computation.10 | convolution fusion | flops 3248488448 | bytes 23855104 | tf_op jit(solution)/shard_map/dot_general | solution.py:46
  128.3 3.1 %fusion.45 = (f32[4,4,32,1024]{3,2,1,0:T(8,128)S(1)}, f32[4,4,32,1024]{3,2,1,0:T(8,128)}, f32[4,4,32,1024]{3,2,1,0:T(8,128)}, f32[4,4,32,1024]{3,2,1,0:T(8,128)S(1)}) fusion(f32[4,4,32,4096]{3,2,1,0:T(8,128)S(1)} %bitcast.97), kind=kLoop, calls=%fused_computation.91 | loop fusion | bytes 16777216 | tf_op jit(solution)/shard_map/slice | solution.py:94
  131.3 1.4 copy-done.2
  132.7 0.9 dynamic-slice_bitcast_fusion.7
  133.6 1.5 collective-permute-start.2
  135.0 1.8 collective-permute-start.1
  136.8 1.3 dynamic-slice_bitcast_fusion.3
  138.1 2.8 %collective-permute-start.13 = (f32[4,32,1024]{2,1,0:T(8,128)S(1)}, f32[4,32,1024]{2,1,0:T(8,128)S(1)}, u32[]{:S(2)}, u32[]{:S(2)}) collective-permute-start(f32[4,32,1024]{2,1,0:T(8,128)S(1)} %get-tuple-element.24), channel_id=1, source_target_pairs={{0,3},{1,0},{2,1},{3,2},{4,7},{5,4},{6,5},{7,6},{8,11},{9,8},{10,9... | collective-permute-start | bytes 1572872 | tf_op jit(solution)/shard_map/ppermute | solution.py:73
  141.0 3.3 %collective-permute-start.20 = (f32[4,32,1024]{2,1,0:T(8,128)S(1)}, f32[4,32,1024]{2,1,0:T(8,128)S(1)}, u32[]{:S(2)}, u32[]{:S(2)}) collective-permute-start(f32[4,32,1024]{2,1,0:T(8,128)S(1)} %get-tuple-element.27), channel_id=1, source_target_pairs={{0,3},{1,0},{2,1},{3,2},{4,7},{5,4},{6,5},{7,6},{8,11},{9,8},{10,9... | collective-permute-start | bytes 1572872 | tf_op jit(solution)/shard_map/ppermute | solution.py:72
  144.4 4.9 %collective-permute-done.2 = f32[4,32,1024]{2,1,0:T(8,128)S(1)} collective-permute-done((f32[4,32,1024]{2,1,0:T(8,128)}, f32[4,32,1024]{2,1,0:T(8,128)S(1)}, u32[]{:S(2)}, u32[]{:S(2)}) %collective-permute-start.2) | collective-permute-done | bytes 524320 | tf_op jit(solution)/shard_map/ppermute | solution.py:72
  149.3 1.5 collective-permute-start.8
  150.9 4.7 %collective-permute-done.14 = f32[4,32,1024]{2,1,0:T(8,128)S(1)} collective-permute-done((f32[4,32,1024]{2,1,0:T(8,128)S(1)}, f32[4,32,1024]{2,1,0:T(8,128)S(1)}, u32[]{:S(2)}, u32[]{:S(2)}) %collective-permute-start.14) | collective-permute-done | bytes 524320 | tf_op jit(solution)/shard_map/ppermute | solution.py:72
  155.6 7.7 %collective-permute-done.20 = f32[4,32,1024]{2,1,0:T(8,128)S(1)} collective-permute-done((f32[4,32,1024]{2,1,0:T(8,128)S(1)}, f32[4,32,1024]{2,1,0:T(8,128)S(1)}, u32[]{:S(2)}, u32[]{:S(2)}) %collective-permute-start.20) | collective-permute-done | bytes 524320 | tf_op jit(solution)/shard_map/ppermute | solution.py:72
  163.4 1.2 collective-permute-start.19
  164.7 1.6 collective-permute-start.15
  166.4 3.7 %collective-permute-done.3 = f32[4,32,1024]{2,1,0:T(8,128)S(1)} collective-permute-done((f32[4,32,1024]{2,1,0:T(8,128)S(1)}, f32[4,32,1024]{2,1,0:T(8,128)S(1)}, u32[]{:S(2)}, u32[]{:S(2)}) %collective-permute-start.3) | collective-permute-done | bytes 524320 | tf_op jit(solution)/shard_map/ppermute | solution.py:74
  170.2 1.4 collective-permute-start.9
  171.6 17.9 %collective-permute-done.15 = f32[4,32,1024]{2,1,0:T(8,128)S(1)} collective-permute-done((f32[4,32,1024]{2,1,0:T(8,128)S(1)}, f32[4,32,1024]{2,1,0:T(8,128)S(1)}, u32[]{:S(2)}, u32[]{:S(2)}) %collective-permute-start.15) | collective-permute-done | bytes 524320 | tf_op jit(solution)/shard_map/ppermute | solution.py:74
  189.5 1.7 collective-permute-start.4
  191.4 0.4 collective-permute-start.5
  191.7 0.7 collective-permute-start.16
  192.6 1.4 collective-permute-start.17
  194.2 3.4 %collective-permute-done.5 = f32[32,1024]{1,0:T(8,128)S(1)} collective-permute-done((f32[32,1024]{1,0:T(8,128)S(1)}, f32[32,1024]{1,0:T(8,128)S(1)}, u32[]{:S(2)}, u32[]{:S(2)}) %collective-permute-start.5) | collective-permute-done | bytes 131104 | tf_op jit(solution)/shard_map/ppermute | solution.py:72
  197.6 0.7 collective-permute-start.23
  198.3 0.5 collective-permute-done.17
  198.8 0.3 collective-permute-start.10
  199.2 3.4 %collective-permute-done.23 = f32[32,1024]{1,0:T(8,128)S(1)} collective-permute-done((f32[32,1024]{1,0:T(8,128)S(1)}, f32[32,1024]{1,0:T(8,128)S(1)}, u32[]{:S(2)}, u32[]{:S(2)}) %collective-permute-start.23) | collective-permute-done | bytes 131104 | tf_op jit(solution)/shard_map/ppermute | solution.py:72
  202.6 0.3 collective-permute-start.11
  202.9 4.6 %collective-permute-done.11 = f32[32,1024]{1,0:T(8,128)S(1)} collective-permute-done((f32[32,1024]{1,0:T(8,128)S(1)}, f32[32,1024]{1,0:T(8,128)S(1)}, u32[]{:S(2)}, u32[]{:S(2)}) %collective-permute-start.11) | collective-permute-done | bytes 131104 | tf_op jit(solution)/shard_map/ppermute | solution.py:72
  207.7 6.1 %collective-permute-done.6 = f32[32,1024]{1,0:T(8,128)S(1)} collective-permute-done((f32[32,1024]{1,0:T(8,128)S(1)}, f32[32,1024]{1,0:T(8,128)S(1)}, u32[]{:S(2)}, u32[]{:S(2)}) %collective-permute-start.6) | collective-permute-done | bytes 131104 | tf_op jit(solution)/shard_map/ppermute | solution.py:74
  213.7 2.0 collective-permute-start.24
  215.7 2.1 collective-permute-start.12
  217.8 0.8 collective-permute-done.24
  218.7 2.0 collective-permute-done.12
  220.9 1.6 collective-permute-start.26
  222.5 1.7 collective-permute-start.25
  224.2 2.9 %collective-permute-done.26 = f32[32,1024]{1,0:T(8,128)S(1)} collective-permute-done((f32[32,1024]{1,0:T(8,128)S(1)}, f32[32,1024]{1,0:T(8,128)S(1)}, u32[]{:S(2)}, u32[]{:S(2)}) %collective-permute-start.26) | collective-permute-done | bytes 131104 | tf_op jit(solution)/shard_map/ppermute | solution.py:60
  227.1 0.4 collective-permute-start.27
  227.5 5.8 %collective-permute-done.27 = f32[32,1024]{1,0:T(8,128)S(1)} collective-permute-done((f32[32,1024]{1,0:T(8,128)S(1)}, f32[32,1024]{1,0:T(8,128)S(1)}, u32[]{:S(2)}, u32[]{:S(2)}) %collective-permute-start.27) | collective-permute-done | bytes 131104 | tf_op jit(solution)/shard_map/ppermute | solution.py:62
  233.4 0.7 add_convert_fusion
  (79 shorter events, 1.8 us)
Async XLA Ops:
  7.2 76.1 %all-gather.2.cloned.1.call-start = ((), (), s32[]{:S(2)}) async-start(), calls=%async_computation | async-start | bytes 8912896 | tf_op jit(solution)/shard_map/all_gather | solution.py:23
  8.7 77.0 %copy-start.11 = (s32[768]{0:T(1024)S(1)}, s32[768]{0:T(1024)}, u32[]{:S(2)}) copy-start(s32[768]{0:T(1024)} %param.8) | copy-start | bytes 9220
  8.7 77.0 %copy-start.12 = (f32[768]{0:T(1024)S(1)}, f32[768]{0:T(1024)}, u32[]{:S(2)}) copy-start(f32[768]{0:T(1024)} %param.9) | copy-start | bytes 9220
  8.7 77.0 %copy-start.13 = (f32[768]{0:T(1024)S(1)}, f32[768]{0:T(1024)}, u32[]{:S(2)}) copy-start(f32[768]{0:T(1024)} %param.10) | copy-start | bytes 9220
  85.8 12.4 %copy-start.7 = (bf16[768,1024]{1,0:T(8,128)(2,1)S(1)}, bf16[768,1024]{1,0:T(8,128)(2,1)}, u32[]{:S(2)}) copy-start(bf16[768,1024]{1,0:T(8,128)(2,1)} %get-tuple-element.10) | copy-start | bytes 4718596
  85.8 12.4 %copy-start.8 = (bf16[768,1024]{1,0:T(8,128)(2,1)S(1)}, bf16[768,1024]{1,0:T(8,128)(2,1)}, u32[]{:S(2)}) copy-start(bf16[768,1024]{1,0:T(8,128)(2,1)} %get-tuple-element.11) | copy-start | bytes 4718596
  85.8 12.4 %copy-start.9 = (bf16[768,1024]{1,0:T(8,128)(2,1)S(1)}, bf16[768,1024]{1,0:T(8,128)(2,1)}, u32[]{:S(2)}) copy-start(bf16[768,1024]{1,0:T(8,128)(2,1)} %get-tuple-element.12) | copy-start | bytes 4718596
  85.8 12.4 %copy-start.10 = (bf16[768,1024]{1,0:T(8,128)(2,1)S(1)}, bf16[768,1024]{1,0:T(8,128)(2,1)}, u32[]{:S(2)}) copy-start(bf16[768,1024]{1,0:T(8,128)(2,1)} %get-tuple-element.13) | copy-start | bytes 4718596
  98.2 7.3 %copy-start.14 = (f32[768,512]{1,0:T(8,128)}, f32[768,512]{1,0:T(8,128)S(1)}, u32[]{:S(2)}) copy-start(f32[768,512]{1,0:T(8,128)S(1)} %get-tuple-element.39) | copy-start | bytes 4718596
  105.5 13.9 %collective-permute-start = (f32[512,4096]{1,0:T(8,128)}, f32[512,4096]{1,0:T(8,128)}, u32[]{:S(2)}, u32[]{:S(2)}) collective-permute-start(f32[512,4096]{1,0:T(8,128)} %fusion), channel_id=1, source_target_pairs={{0,16},{16,0},{32,48},{48,32},{64,80},{80,64},{96,112},{112,96},{1... | collective-permute-start | bytes 25165832 | tf_op jit(solution)/shard_map/ppermute | solution.py:43
  105.5 13.9 %copy-start.4 = (bf16[768,1024]{1,0:T(8,128)(2,1)S(1)}, bf16[768,1024]{1,0:T(8,128)(2,1)}, u32[]{:S(2)}) copy-start(bf16[768,1024]{1,0:T(8,128)(2,1)} %get-tuple-element.9) | copy-start | bytes 4718596
  105.5 13.9 %copy-start.5 = (bf16[768,1024]{1,0:T(8,128)(2,1)S(1)}, bf16[768,1024]{1,0:T(8,128)(2,1)}, u32[]{:S(2)}) copy-start(bf16[768,1024]{1,0:T(8,128)(2,1)} %get-tuple-element.14) | copy-start | bytes 4718596
  105.5 13.9 %copy-start.6 = (bf16[768,1024]{1,0:T(8,128)(2,1)S(1)}, bf16[768,1024]{1,0:T(8,128)(2,1)}, u32[]{:S(2)}) copy-start(bf16[768,1024]{1,0:T(8,128)(2,1)} %get-tuple-element.15) | copy-start | bytes 4718596
  131.3 1.4 copy-start.2
  133.6 15.7 %collective-permute-start.2 = (f32[4,32,1024]{2,1,0:T(8,128)}, f32[4,32,1024]{2,1,0:T(8,128)S(1)}, u32[]{:S(2)}, u32[]{:S(2)}) collective-permute-start(f32[4,32,1024]{2,1,0:T(8,128)} %get-tuple-element.21), channel_id=1, source_target_pairs={{0,4},{1,5},{2,6},{3,7},{4,8},{5,9},{6,10},{7,11},{8,12},{9,13},{1... | collective-permute-start | bytes 1572872 | tf_op jit(solution)/shard_map/ppermute | solution.py:72
  135.0 5.9 %copy-start = (f32[4,4,32,1024]{3,2,1,0:T(8,128)S(1)}, f32[4,4,32,1024]{3,2,1,0:T(8,128)}, u32[]{:S(2)}) copy-start(f32[4,4,32,1024]{3,2,1,0:T(8,128)} %get-tuple-element.17) | copy-start | bytes 6291460
  135.0 31.3 %collective-permute-start.1 = (f32[4,32,1024]{2,1,0:T(8,128)S(1)}, f32[4,32,1024]{2,1,0:T(8,128)S(1)}, u32[]{:S(2)}, u32[]{:S(2)}) collective-permute-start(f32[4,32,1024]{2,1,0:T(8,128)S(1)} %get-tuple-element.20), channel_id=1, source_target_pairs={{0,12},{1,13},{2,14},{3,15},{4,0},{5,1},{6,2},{7,3},{8,4},{9,5},{1... | collective-permute-start | bytes 1572872 | tf_op jit(solution)/shard_map/ppermute | solution.py:73
  138.1 32.1 %collective-permute-start.13 = (f32[4,32,1024]{2,1,0:T(8,128)S(1)}, f32[4,32,1024]{2,1,0:T(8,128)S(1)}, u32[]{:S(2)}, u32[]{:S(2)}) collective-permute-start(f32[4,32,1024]{2,1,0:T(8,128)S(1)} %get-tuple-element.24), channel_id=1, source_target_pairs={{0,3},{1,0},{2,1},{3,2},{4,7},{5,4},{6,5},{7,6},{8,11},{9,8},{10,9... | collective-permute-start | bytes 1572872 | tf_op jit(solution)/shard_map/ppermute | solution.py:73
  140.9 14.7 %collective-permute-start.14 = (f32[4,32,1024]{2,1,0:T(8,128)S(1)}, f32[4,32,1024]{2,1,0:T(8,128)S(1)}, u32[]{:S(2)}, u32[]{:S(2)}) collective-permute-start(f32[4,32,1024]{2,1,0:T(8,128)S(1)} %get-tuple-element.25), channel_id=1, source_target_pairs={{0,1},{1,2},{2,3},{3,0},{4,5},{5,6},{6,7},{7,4},{8,9},{9,10},{10,1... | collective-permute-start | bytes 1572872 | tf_op jit(solution)/shard_map/ppermute | solution.py:72
  140.9 9.9 %copy-start.3 = (f32[4,4,32,1024]{3,2,1,0:T(8,128)S(1)}, f32[4,4,32,1024]{3,2,1,0:T(8,128)}, u32[]{:S(2)}) copy-start(f32[4,4,32,1024]{3,2,1,0:T(8,128)} %copy-done.2) | copy-start | bytes 6291460
  141.0 22.4 %collective-permute-start.20 = (f32[4,32,1024]{2,1,0:T(8,128)S(1)}, f32[4,32,1024]{2,1,0:T(8,128)S(1)}, u32[]{:S(2)}, u32[]{:S(2)}) collective-permute-start(f32[4,32,1024]{2,1,0:T(8,128)S(1)} %get-tuple-element.27), channel_id=1, source_target_pairs={{0,3},{1,0},{2,1},{3,2},{4,7},{5,4},{6,5},{7,6},{8,11},{9,8},{10,9... | collective-permute-start | bytes 1572872 | tf_op jit(solution)/shard_map/ppermute | solution.py:72
  144.3 11.3 %copy-start.1 = (f32[4,4,32,1024]{3,2,1,0:T(8,128)S(1)}, f32[4,4,32,1024]{3,2,1,0:T(8,128)}, u32[]{:S(2)}) copy-start(f32[4,4,32,1024]{3,2,1,0:T(8,128)} %get-tuple-element.18) | copy-start | bytes 6291460
  149.3 15.3 %collective-permute-start.8 = (f32[4,32,1024]{2,1,0:T(8,128)S(1)}, f32[4,32,1024]{2,1,0:T(8,128)S(1)}, u32[]{:S(2)}, u32[]{:S(2)}) collective-permute-start(f32[4,32,1024]{2,1,0:T(8,128)S(1)} %get-tuple-element.23), channel_id=1, source_target_pairs={{0,12},{1,13},{2,14},{3,15},{4,0},{5,1},{6,2},{7,3},{8,4},{9,5},{1... | collective-permute-start | bytes 1572872 | tf_op jit(solution)/shard_map/ppermute | solution.py:72
  155.6 14.5 %collective-permute-start.3 = (f32[4,32,1024]{2,1,0:T(8,128)S(1)}, f32[4,32,1024]{2,1,0:T(8,128)S(1)}, u32[]{:S(2)}, u32[]{:S(2)}) collective-permute-start(f32[4,32,1024]{2,1,0:T(8,128)S(1)} %bitcast_add_fusion.6), channel_id=1, source_target_pairs={{0,4},{1,5},{2,6},{3,7},{4,8},{5,9},{6,10},{7,11},{8,12},{9,13},{1... | collective-permute-start | bytes 1572872 | tf_op jit(solution)/shard_map/ppermute | solution.py:74
  163.4 28.0 %collective-permute-start.19 = (f32[4,32,1024]{2,1,0:T(8,128)S(1)}, f32[4,32,1024]{2,1,0:T(8,128)S(1)}, u32[]{:S(2)}, u32[]{:S(2)}) collective-permute-start(f32[4,32,1024]{2,1,0:T(8,128)S(1)} %get-tuple-element.26), channel_id=1, source_target_pairs={{0,1},{1,2},{2,3},{3,0},{4,5},{5,6},{6,7},{7,4},{8,9},{9,10},{10,1... | collective-permute-start | bytes 1572872 | tf_op jit(solution)/shard_map/ppermute | solution.py:73
  164.7 24.8 %collective-permute-start.15 = (f32[4,32,1024]{2,1,0:T(8,128)S(1)}, f32[4,32,1024]{2,1,0:T(8,128)S(1)}, u32[]{:S(2)}, u32[]{:S(2)}) collective-permute-start(f32[4,32,1024]{2,1,0:T(8,128)S(1)} %bitcast_add_fusion.2), channel_id=1, source_target_pairs={{0,1},{1,2},{2,3},{3,0},{4,5},{5,6},{6,7},{7,4},{8,9},{9,10},{10,1... | collective-permute-start | bytes 1572872 | tf_op jit(solution)/shard_map/ppermute | solution.py:74
  166.3 26.3 %collective-permute-start.7 = (f32[4,32,1024]{2,1,0:T(8,128)S(1)}, f32[4,32,1024]{2,1,0:T(8,128)S(1)}, u32[]{:S(2)}, u32[]{:S(2)}) collective-permute-start(f32[4,32,1024]{2,1,0:T(8,128)S(1)} %get-tuple-element.22), channel_id=1, source_target_pairs={{0,4},{1,5},{2,6},{3,7},{4,8},{5,9},{6,10},{7,11},{8,12},{9,13},{1... | collective-permute-start | bytes 1572872 | tf_op jit(solution)/shard_map/ppermute | solution.py:73
  170.1 21.6 %collective-permute-start.21 = (f32[4,32,1024]{2,1,0:T(8,128)S(1)}, f32[4,32,1024]{2,1,0:T(8,128)S(1)}, u32[]{:S(2)}, u32[]{:S(2)}) collective-permute-start(f32[4,32,1024]{2,1,0:T(8,128)S(1)} %bitcast_add_fusion), channel_id=1, source_target_pairs={{0,3},{1,0},{2,1},{3,2},{4,7},{5,4},{6,5},{7,6},{8,11},{9,8},{10,9... | collective-permute-start | bytes 1572872 | tf_op jit(solution)/shard_map/ppermute | solution.py:74
  170.2 23.8 %collective-permute-start.9 = (f32[4,32,1024]{2,1,0:T(8,128)S(1)}, f32[4,32,1024]{2,1,0:T(8,128)S(1)}, u32[]{:S(2)}, u32[]{:S(2)}) collective-permute-start(f32[4,32,1024]{2,1,0:T(8,128)S(1)} %bitcast_add_fusion.4), channel_id=1, source_target_pairs={{0,12},{1,13},{2,14},{3,15},{4,0},{5,1},{6,2},{7,3},{8,4},{9,5},{1... | collective-permute-start | bytes 1572872 | tf_op jit(solution)/shard_map/ppermute | solution.py:74
  189.5 18.1 %collective-permute-start.4 = (f32[32,1024]{1,0:T(8,128)S(1)}, f32[32,1024]{1,0:T(8,128)S(1)}, u32[]{:S(2)}, u32[]{:S(2)}) collective-permute-start(f32[32,1024]{1,0:T(8,128)S(1)} %get-tuple-element.30), channel_id=1, source_target_pairs={{0,3},{1,0},{2,1},{3,2},{4,7},{5,4},{6,5},{7,6},{8,11},{9,8},{10,9... | collective-permute-start | bytes 393224 | tf_op jit(solution)/shard_map/ppermute | solution.py:73
  191.4 6.2 %collective-permute-start.5 = (f32[32,1024]{1,0:T(8,128)S(1)}, f32[32,1024]{1,0:T(8,128)S(1)}, u32[]{:S(2)}, u32[]{:S(2)}) collective-permute-start(f32[32,1024]{1,0:T(8,128)S(1)} %get-tuple-element.31), channel_id=1, source_target_pairs={{0,1},{1,2},{2,3},{3,0},{4,5},{5,6},{6,7},{7,4},{8,9},{9,10},{10,1... | collective-permute-start | bytes 393224 | tf_op jit(solution)/shard_map/ppermute | solution.py:72
  191.7 24.0 %collective-permute-start.16 = (f32[32,1024]{1,0:T(8,128)S(1)}, f32[32,1024]{1,0:T(8,128)S(1)}, u32[]{:S(2)}, u32[]{:S(2)}) collective-permute-start(f32[32,1024]{1,0:T(8,128)S(1)} %get-tuple-element.34), channel_id=1, source_target_pairs={{0,12},{1,13},{2,14},{3,15},{4,0},{5,1},{6,2},{7,3},{8,4},{9,5},{1... | collective-permute-start | bytes 393224 | tf_op jit(solution)/shard_map/ppermute | solution.py:73
  192.6 6.2 %collective-permute-start.17 = (f32[32,1024]{1,0:T(8,128)S(1)}, f32[32,1024]{1,0:T(8,128)S(1)}, u32[]{:S(2)}, u32[]{:S(2)}) collective-permute-start(f32[32,1024]{1,0:T(8,128)S(1)} %get-tuple-element.35), channel_id=1, source_target_pairs={{0,4},{1,5},{2,6},{3,7},{4,8},{5,9},{6,10},{7,11},{8,12},{9,13},{1... | collective-permute-start | bytes 393224 | tf_op jit(solution)/shard_map/ppermute | solution.py:72
  194.0 23.9 %collective-permute-start.22 = (f32[32,1024]{1,0:T(8,128)S(1)}, f32[32,1024]{1,0:T(8,128)S(1)}, u32[]{:S(2)}, u32[]{:S(2)}) collective-permute-start(f32[32,1024]{1,0:T(8,128)S(1)} %get-tuple-element.36), channel_id=1, source_target_pairs={{0,4},{1,5},{2,6},{3,7},{4,8},{5,9},{6,10},{7,11},{8,12},{9,13},{1... | collective-permute-start | bytes 393224 | tf_op jit(solution)/shard_map/ppermute | solution.py:73
  197.6 5.0 %collective-permute-start.23 = (f32[32,1024]{1,0:T(8,128)S(1)}, f32[32,1024]{1,0:T(8,128)S(1)}, u32[]{:S(2)}, u32[]{:S(2)}) collective-permute-start(f32[32,1024]{1,0:T(8,128)S(1)} %get-tuple-element.37), channel_id=1, source_target_pairs={{0,12},{1,13},{2,14},{3,15},{4,0},{5,1},{6,2},{7,3},{8,4},{9,5},{1... | collective-permute-start | bytes 393224 | tf_op jit(solution)/shard_map/ppermute | solution.py:72
  198.8 19.9 %collective-permute-start.10 = (f32[32,1024]{1,0:T(8,128)S(1)}, f32[32,1024]{1,0:T(8,128)S(1)}, u32[]{:S(2)}, u32[]{:S(2)}) collective-permute-start(f32[32,1024]{1,0:T(8,128)S(1)} %get-tuple-element.32), channel_id=1, source_target_pairs={{0,1},{1,2},{2,3},{3,0},{4,5},{5,6},{6,7},{7,4},{8,9},{9,10},{10,1... | collective-permute-start | bytes 393224 | tf_op jit(solution)/shard_map/ppermute | solution.py:73
  202.6 5.0 %collective-permute-start.11 = (f32[32,1024]{1,0:T(8,128)S(1)}, f32[32,1024]{1,0:T(8,128)S(1)}, u32[]{:S(2)}, u32[]{:S(2)}) collective-permute-start(f32[32,1024]{1,0:T(8,128)S(1)} %get-tuple-element.33), channel_id=1, source_target_pairs={{0,3},{1,0},{2,1},{3,2},{4,7},{5,4},{6,5},{7,6},{8,11},{9,8},{10,9... | collective-permute-start | bytes 393224 | tf_op jit(solution)/shard_map/ppermute | solution.py:72
  207.5 6.2 %collective-permute-start.6 = (f32[32,1024]{1,0:T(8,128)S(1)}, f32[32,1024]{1,0:T(8,128)S(1)}, u32[]{:S(2)}, u32[]{:S(2)}) collective-permute-start(f32[32,1024]{1,0:T(8,128)S(1)} %bitcast_add_fusion.14), channel_id=1, source_target_pairs={{0,1},{1,2},{2,3},{3,0},{4,5},{5,6},{6,7},{7,4},{8,9},{9,10},{10,1... | collective-permute-start | bytes 393224 | tf_op jit(solution)/shard_map/ppermute | solution.py:74
  207.6 10.2 %collective-permute-start.18 = (f32[32,1024]{1,0:T(8,128)S(1)}, f32[32,1024]{1,0:T(8,128)S(1)}, u32[]{:S(2)}, u32[]{:S(2)}) collective-permute-start(f32[32,1024]{1,0:T(8,128)S(1)} %bitcast_add_fusion.10), channel_id=1, source_target_pairs={{0,4},{1,5},{2,6},{3,7},{4,8},{5,9},{6,10},{7,11},{8,12},{9,13},{1... | collective-permute-start | bytes 393224 | tf_op jit(solution)/shard_map/ppermute | solution.py:74
  213.7 5.0 %collective-permute-start.24 = (f32[32,1024]{1,0:T(8,128)S(1)}, f32[32,1024]{1,0:T(8,128)S(1)}, u32[]{:S(2)}, u32[]{:S(2)}) collective-permute-start(f32[32,1024]{1,0:T(8,128)S(1)} %bitcast_add_fusion.8), channel_id=1, source_target_pairs={{0,12},{1,13},{2,14},{3,15},{4,0},{5,1},{6,2},{7,3},{8,4},{9,5},{1... | collective-permute-start | bytes 393224 | tf_op jit(solution)/shard_map/ppermute | solution.py:74
  215.7 5.0 %collective-permute-start.12 = (f32[32,1024]{1,0:T(8,128)S(1)}, f32[32,1024]{1,0:T(8,128)S(1)}, u32[]{:S(2)}, u32[]{:S(2)}) collective-permute-start(f32[32,1024]{1,0:T(8,128)S(1)} %bitcast_add_fusion.12), channel_id=1, source_target_pairs={{0,3},{1,0},{2,1},{3,2},{4,7},{5,4},{6,5},{7,6},{8,11},{9,8},{10,9... | collective-permute-start | bytes 393224 | tf_op jit(solution)/shard_map/ppermute | solution.py:74
  220.9 6.2 %collective-permute-start.26 = (f32[32,1024]{1,0:T(8,128)S(1)}, f32[32,1024]{1,0:T(8,128)S(1)}, u32[]{:S(2)}, u32[]{:S(2)}) collective-permute-start(f32[32,1024]{1,0:T(8,128)S(1)} %get-tuple-element.29), channel_id=1, source_target_pairs={{0,32},{16,48},{32,64},{48,80},{64,96},{80,112},{96,0},{112,16},{1... | collective-permute-start | bytes 393224 | tf_op jit(solution)/shard_map/ppermute | solution.py:60
  222.5 5.1 %collective-permute-start.25 = (f32[32,1024]{1,0:T(8,128)S(1)}, f32[32,1024]{1,0:T(8,128)S(1)}, u32[]{:S(2)}, u32[]{:S(2)}) collective-permute-start(f32[32,1024]{1,0:T(8,128)S(1)} %get-tuple-element.28), channel_id=1, source_target_pairs={{0,96},{16,112},{32,0},{48,16},{64,32},{80,48},{96,64},{112,80},{1... | collective-permute-start | bytes 393224 | tf_op jit(solution)/shard_map/ppermute | solution.py:61
  227.1 6.2 %collective-permute-start.27 = (f32[32,1024]{1,0:T(8,128)S(1)}, f32[32,1024]{1,0:T(8,128)S(1)}, u32[]{:S(2)}, u32[]{:S(2)}) collective-permute-start(f32[32,1024]{1,0:T(8,128)S(1)} %dynamic-slice_add_fusion), channel_id=1, source_target_pairs={{0,32},{16,48},{32,64},{48,80},{64,96},{80,112},{96,0},{112,16},{1... | collective-permute-start | bytes 393224 | tf_op jit(solution)/shard_map/ppermute | solution.py:62
Sparse Core Ops, SparseCore 0:
  10.1 73.1 all-gather.1
